TPU v7x, 128 devices: a whole 4x4x4 slice. The times are simulated.
128 devices in a mesh: dp: 8 (over z, core), expert: 16 (over y, x).
Axes of the slice: x: 4, y: 4, z: 4, core: 2. Of those that a mesh axis runs over, the one named last changes fastest.
Arguments:
- hidden_in: bfloat16 [16384, 2048], P(('dp', 'expert')), may hold values from -40 to 40, as said below
- norm_gain: float32 [2048], replicated, may hold values from 0.5 to 1.5
- router_weight: bfloat16 [2048, 128], replicated, may hold values from -2 to 2, as said below
- grad_out: bfloat16 [16384, 2048], P(('dp', 'expert')), may hold values from -20 to 20, as said below
- expert_ids: int32 [16384, 8], P(('dp', 'expert')), may hold values from 0 to 127, all different within a row; in each aligned block of 128 rows (0 to 127, 128 to 255, ...) at most 9 rows name the same one
- gate_weight: bfloat16 [128, 2048, 768], P(('dp', 'expert')), may hold values from -0.125 to 0.125
- up_weight: bfloat16 [128, 2048, 768], P(('dp', 'expert')), may hold values from -0.125 to 0.125
- down_weight: bfloat16 [128, 768, 2048], P(('dp', 'expert')), may hold values from -0.21875 to 0.21875
Outputs:
- grad_hidden: bfloat16 [16384, 2048], P(('dp', 'expert'))
- grad_router: float32 [2048, 128], replicated
- grad_gain: float32 [2048], replicated
- grad_gate_weight: bfloat16 [128, 2048, 768], P(('dp', 'expert'))
- grad_up_weight: bfloat16 [128, 2048, 768], P(('dp', 'expert'))
- grad_down_weight: bfloat16 [128, 768, 2048], P(('dp', 'expert'))
Inputs may be any that keep to these rules, and one draw needn't show every extreme that they name: `expert_ids`: each row names 8 different experts. Among the 128 rows of one device no expert is named more than 9 times; in some devices' rows an expert is named exactly 9 times. `hidden_in`: real values. `router_weight`: real values. `grad_out`: real values.
All inputs are finite; a program needn't handle non-finite values.
Results may differ from a plain program's by a relative error of at most 0.0079.
Values may be sent and summed in bfloat16 or wider, within the bound.
No kernel may reach another device: no remote copies, remote signals or barrier semaphores. Data moves between devices by JAX's collectives and lax.ppermute only.
A program may use at most 128 MiB of HBM per device.

v0:
```python
import jax
import jax.numpy as jnp
from jax import lax
from jax.sharding import PartitionSpec as P


def silu_parts(value):
    sigmoid_v = jax.nn.sigmoid(value)
    return (value * sigmoid_v, sigmoid_v * (1.0 + value * (1.0 - sigmoid_v)))


def contract(left, right, left_dim, right_dim):
    return lax.dot_general(
        left, right, (((left_dim,), (right_dim,)), ((), ())), preferred_element_type=jnp.float32
    )


def expert_backward(inputs, upstream, prob_rows, gate_mat, up_mat, down_mat):
    pre_gate = jnp.dot(inputs, gate_mat, preferred_element_type=jnp.float32)
    pre_up = jnp.dot(inputs, up_mat, preferred_element_type=jnp.float32)
    activated, derivative = silu_parts(pre_gate)
    hidden_act = activated * pre_up
    grad_mid = contract(upstream, down_mat, 1, 1)
    route_grad = jnp.sum(grad_mid * hidden_act, axis=1).astype(jnp.bfloat16)
    prob_col = prob_rows.astype(jnp.float32)[:, None]
    scaled = prob_col * grad_mid
    grad_pre_gate = (scaled * pre_up * derivative).astype(jnp.bfloat16)
    grad_pre_up = (scaled * activated).astype(jnp.bfloat16)
    scaled_up = (prob_col * upstream.astype(jnp.float32)).astype(jnp.bfloat16)
    grad_gate_mat = contract(inputs, grad_pre_gate, 0, 0).astype(jnp.bfloat16)
    grad_up_mat = contract(inputs, grad_pre_up, 0, 0).astype(jnp.bfloat16)
    grad_down_mat = contract(hidden_act.astype(jnp.bfloat16), scaled_up, 0, 0).astype(jnp.bfloat16)
    grad_inputs = (
        contract(grad_pre_gate, gate_mat, 1, 1) + contract(grad_pre_up, up_mat, 1, 1)
    ).astype(jnp.bfloat16)
    return (grad_gate_mat, grad_up_mat, grad_down_mat, grad_inputs, route_grad)


def local(
    hidden_in, norm_gain, router_weight, grad_out, expert_ids, gate_weight, up_weight, down_weight
):
    tok_rows, model_width = hidden_in.shape
    top_count = expert_ids.shape[1]
    experts = router_weight.shape[1]
    capacity = max(2, (tok_rows * top_count * 9 + 8 * experts - 1) // (8 * experts))
    routes = tok_rows * top_count
    values = hidden_in.astype(jnp.float32)
    inv_rms = lax.rsqrt(jnp.mean(values * values, axis=1, keepdims=True) + 1e-06)
    normed = (values * inv_rms * norm_gain).astype(jnp.bfloat16)
    logits = jnp.dot(normed, router_weight, preferred_element_type=jnp.float32)
    chosen = expert_ids[:, :, None] == jnp.arange(experts, dtype=jnp.int32)[None, None, :]
    picked = jnp.sum(jnp.where(chosen, logits[:, None, :], 0.0), axis=2)
    route_prob = jax.nn.softmax(picked, axis=1)
    prob_bf = route_prob.astype(jnp.bfloat16)
    flat_ids = expert_ids.reshape(-1)
    onehot = (flat_ids[:, None] == jnp.arange(experts, dtype=jnp.int32)[None, :]).astype(jnp.int32)
    counts = jnp.cumsum(onehot, axis=0)
    slot_idx = jnp.sum(counts * onehot, axis=1) - 1
    target = flat_ids * capacity + slot_idx
    owner_idx = (
        jnp.full((experts * capacity,), routes, jnp.int32)
        .at[target]
        .set(jnp.arange(routes, dtype=jnp.int32))
    )
    token_of = jnp.where(owner_idx < routes, owner_idx // top_count, tok_rows)
    pad_normed = jnp.concatenate([normed, jnp.zeros((1, model_width), jnp.bfloat16)], axis=0)
    pad_grads = jnp.concatenate([grad_out, jnp.zeros((1, model_width), jnp.bfloat16)], axis=0)
    pad_probs = jnp.concatenate([prob_bf.reshape(-1), jnp.zeros((1,), jnp.bfloat16)], axis=0)
    send_rows = pad_normed[token_of].reshape(experts, capacity, model_width)
    send_grads = pad_grads[token_of].reshape(experts, capacity, model_width)
    send_probs = pad_probs[owner_idx].reshape(experts, capacity)
    received_x, received_y, received_p = (
        lax.all_to_all(send_rows, ("dp", "expert"), split_axis=0, concat_axis=0, tiled=True),
        lax.all_to_all(send_grads, ("dp", "expert"), split_axis=0, concat_axis=0, tiled=True),
        lax.all_to_all(send_probs, ("dp", "expert"), split_axis=0, concat_axis=0, tiled=True),
    )
    grad_gate_mat, grad_up_mat, grad_down_mat, grad_inputs, route_grad = expert_backward(
        received_x.reshape(-1, model_width),
        received_y.reshape(-1, model_width),
        received_p.reshape(-1),
        gate_weight[0],
        up_weight[0],
        down_weight[0],
    )
    back_inputs, back_grads = (
        lax.all_to_all(
            grad_inputs.reshape(experts, capacity, model_width),
            ("dp", "expert"),
            split_axis=0,
            concat_axis=0,
            tiled=True,
        ),
        lax.all_to_all(
            route_grad.reshape(experts, capacity),
            ("dp", "expert"),
            split_axis=0,
            concat_axis=0,
            tiled=True,
        ),
    )
    back_rows = back_inputs.reshape(experts * capacity, model_width)[target].reshape(
        tok_rows, top_count, model_width
    )
    route_sum = jnp.sum(back_rows.astype(jnp.float32), axis=1)
    grad_prob = back_grads.reshape(-1)[target].reshape(tok_rows, top_count).astype(jnp.float32)
    grad_picked = route_prob * (grad_prob - jnp.sum(route_prob * grad_prob, axis=1, keepdims=True))
    grad_logit = jnp.sum(jnp.where(chosen, grad_picked[:, :, None], 0.0), axis=1).astype(
        jnp.bfloat16
    )
    router_part = contract(normed, grad_logit, 0, 0)
    grad_normed = route_sum + contract(grad_logit, router_weight, 1, 1)
    gain_part = jnp.sum(grad_normed * values * inv_rms, axis=0)
    grad_router, grad_gain = lax.psum((router_part, gain_part), ("dp", "expert"))
    scaled = norm_gain * grad_normed
    cube = inv_rms * inv_rms * inv_rms
    grad_hidden = (
        grad_out.astype(jnp.float32)
        + inv_rms * scaled
        - values * cube * jnp.mean(scaled * values, axis=1, keepdims=True)
    ).astype(jnp.bfloat16)
    return (
        grad_hidden,
        grad_router,
        grad_gain,
        grad_gate_mat[None],
        grad_up_mat[None],
        grad_down_mat[None],
    )


def solution(mesh):
    in_specs = (
        P(("dp", "expert"), None),
        P(),
        P(),
        P(("dp", "expert"), None),
        P(("dp", "expert"), None),
        P(("dp", "expert"), None, None),
        P(("dp", "expert"), None, None),
        P(("dp", "expert"), None, None),
    )
    out_specs = (
        P(("dp", "expert"), None),
        P(),
        P(),
        P(("dp", "expert"), None, None),
        P(("dp", "expert"), None, None),
        P(("dp", "expert"), None, None),
    )
    return jax.shard_map(local, mesh=mesh, in_specs=in_specs, out_specs=out_specs, check_vma=False)
```

profile of v0, /device:TPU:1, one launch (start us, length us, event | category | flops | bytes accessed | tf_op | source)
XLA Modules:
  0.0 578.4 jit_solution(18355201469567292837)
XLA Ops:
  13.3 4.3 scatter_custom_fusion
  21.9 7.3 %gather_fusion = bf16[1152]{0:T(1024)(128)(2,1)S(1)} fusion(bf16[1025]{0:T(1024)(128)(2,1)S(1)} %pad_maximum_fusion, s32[2048]{0:T(1024)S(1)} %get-tuple-element.17), kind=kCustom, calls=%fused_computation | custom fusion | bytes 9216 | tf_op jit(solution)/shard_map/gather | solution.py:71
  30.1 11.5 %all-to-all-start = ((bf16[128,1,9]{2,1,0:T(2,128)(2,1)}), bf16[128,1,9]{2,1,0:T(2,128)(2,1)S(1)}, u32[]{:S(2)}, u32[]{:S(2)}) async-start(bf16[128,1,9]{2,1,0:T(2,128)(2,1)} %all_to_all.25), calls=%async_computation | async-start | bytes 131072 | tf_op jit(solution)/shard_map/all_to_all | solution.py:75
  43.5 11.8 %gather_fusion.2 = bf16[1152,2048]{1,0:T(8,128)(2,1)} fusion(bf16[129,2048]{1,0:T(8,128)(2,1)} %concatenate.11, s32[2048]{0:T(1024)S(1)} %get-tuple-element.16), kind=kCustom, calls=%fused_computation.2 | custom fusion | bytes 9441792 | tf_op jit(solution)/shard_map/gather | solution.py:69
  55.3 8.1 %reshape.206 = bf16[128,9,2048]{2,1,0:T(8,128)(2,1)} reshape(bf16[1152,2048]{1,0:T(8,128)(2,1)} %gather_fusion.2) | data formatting | bytes 9437184 | tf_op jit(solution)/shard_map/reshape | solution.py:69
  63.4 10.2 %all-to-all-start.2 = ((bf16[128,9,2048]{2,1,0:T(8,128)(2,1)}), bf16[128,9,2048]{2,1,0:T(8,128)(2,1)}, u32[]{:S(2)}, u32[]{:S(2)}) async-start(bf16[128,9,2048]{2,1,0:T(8,128)(2,1)} %reshape.206), calls=%async_computation.2 | async-start | bytes 16777216 | tf_op jit(solution)/shard_map/all_to_all | solution.py:73
  75.5 11.8 %gather_fusion.1 = bf16[1152,2048]{1,0:T(8,128)(2,1)} fusion(bf16[129,2048]{1,0:T(8,128)(2,1)} %concatenate.10, s32[2048]{0:T(1024)S(1)} %get-tuple-element.16), kind=kCustom, calls=%fused_computation.1 | custom fusion | bytes 9441792 | tf_op jit(solution)/shard_map/gather | solution.py:70
  87.4 8.0 %reshape.204 = bf16[128,9,2048]{2,1,0:T(8,128)(2,1)} reshape(bf16[1152,2048]{1,0:T(8,128)(2,1)} %gather_fusion.1) | data formatting | bytes 9437184 | tf_op jit(solution)/shard_map/reshape | solution.py:70
  95.4 75.9 %all-to-all-done.2 = bf16[128,9,2048]{2,1,0:T(8,128)(2,1)} async-done(((bf16[128,9,2048]{2,1,0:T(8,128)(2,1)}), bf16[128,9,2048]{2,1,0:T(8,128)(2,1)}, u32[]{:S(2)}, u32[]{:S(2)}) %all-to-all-start.2) | async-done | bytes 4718624 | tf_op jit(solution)/shard_map/all_to_all | solution.py:73
  171.3 14.3 %all-to-all-start.1 = ((bf16[128,9,2048]{2,1,0:T(8,128)(2,1)}), bf16[128,9,2048]{2,1,0:T(8,128)(2,1)}, u32[]{:S(2)}, u32[]{:S(2)}) async-start(bf16[128,9,2048]{2,1,0:T(8,128)(2,1)} %reshape.204), calls=%async_computation.1 | async-start | bytes 16777216 | tf_op jit(solution)/shard_map/all_to_all | solution.py:74
  186.0 8.4 %reshape.207 = bf16[1152,2048]{1,0:T(8,128)(2,1)} reshape(bf16[128,9,2048]{2,1,0:T(8,128)(2,1)} %all-to-all-done.2) | data formatting | bytes 9437184 | tf_op jit(solution)/shard_map/reshape | solution.py:78
  194.4 8.5 %fusion.6 = f32[1152,768]{0,1:T(8,128)} fusion(bf16[1152,2048]{1,0:T(8,128)(2,1)} %reshape.207, bf16[1,2048,768]{2,1,0:T(8,128)(2,1)S(1)} %copy-done), kind=kOutput, calls=%fused_computation.21 | convolution fusion | flops 3623878656 | bytes 11403264 | tf_op jit(solution)/shard_map/dot_general | solution.py:19
  202.9 6.3 %fusion.9 = f32[1152,768]{0,1:T(8,128)} fusion(bf16[1152,2048]{1,0:T(8,128)(2,1)S(1)} %copy-done.5, bf16[1,2048,768]{2,1,0:T(8,128)(2,1)S(1)} %copy-done.9), kind=kOutput, calls=%fused_computation.24 | convolution fusion | flops 3623878656 | bytes 11403264 | tf_op jit(solution)/shard_map/dot_general | solution.py:20
  209.2 73.6 %all-to-all-done.1 = bf16[128,9,2048]{2,1,0:T(8,128)(2,1)} async-done(((bf16[128,9,2048]{2,1,0:T(8,128)(2,1)}), bf16[128,9,2048]{2,1,0:T(8,128)(2,1)}, u32[]{:S(2)}, u32[]{:S(2)}) %all-to-all-start.1) | async-done | bytes 4718624 | tf_op jit(solution)/shard_map/all_to_all | solution.py:74
  282.9 8.7 %reshape.205 = bf16[1152,2048]{1,0:T(8,128)(2,1)} reshape(bf16[128,9,2048]{2,1,0:T(8,128)(2,1)} %all-to-all-done.1) | data formatting | bytes 9437184 | tf_op jit(solution)/shard_map/reshape | solution.py:79
  291.6 12.6 %multiply_reduce_fusion = (bf16[1152]{0:T(1024)(128)(2,1)S(1)}, bf16[1152,768]{0,1:T(8,128)(2,1)}, bf16[1152,768]{0,1:T(8,128)(2,1)}) fusion(f32[1152,768]{0,1:T(8,128)} %fusion.9, f32[1152,768]{0,1:T(8,128)} %fusion.6, f32[1152]{0:T(1024)S(1)} %reshape.211, bf16[1152,2048]{1,0:T(8,128)(2,1)} %reshape.205, bf16[1,768,2048]{2,1,0:T(8,128)(2,1)} %param.15), kind=kOutput, calls=%fused_computation.11 | convolution fusion | flops 3638918144 | bytes 18488064 | tf_op jit(solution)/shard_map/dot_general | solution.py:13
  305.0 12.6 %all-to-all-start.4 = ((bf16[128,1,9]{2,1,0:T(2,128)(2,1)}), bf16[128,1,9]{2,1,0:T(2,128)(2,1)S(1)}, u32[]{:S(2)}, u32[]{:S(2)}) async-start(bf16[128,1,9]{2,1,0:T(2,128)(2,1)} %convert_element_type.122), calls=%async_computation.4 | async-start | bytes 131072 | tf_op jit(solution)/shard_map/all_to_all | solution.py:93
  317.6 5.6 fusion.4
  323.2 5.7 add_convert_fusion
  328.9 8.1 %reshape.208 = bf16[128,9,2048]{2,1,0:T(8,128)(2,1)} reshape(bf16[1152,2048]{1,0:T(8,128)(2,1)} %add_convert_fusion) | data formatting | bytes 9437184 | tf_op jit(solution)/shard_map/reshape | solution.py:87
  337.1 10.2 %all-to-all-start.3 = ((bf16[128,9,2048]{2,1,0:T(8,128)(2,1)}), bf16[128,9,2048]{2,1,0:T(8,128)(2,1)}, u32[]{:S(2)}, u32[]{:S(2)}) async-start(bf16[128,9,2048]{2,1,0:T(8,128)(2,1)} %reshape.208), calls=%async_computation.3 | async-start | bytes 16777216 | tf_op jit(solution)/shard_map/all_to_all | solution.py:86
  347.4 8.5 %fusion.13 = bf16[1,2048,768]{2,1,0:T(8,128)(2,1)} fusion(bf16[1152,2048]{1,0:T(8,128)(2,1)} %reshape.207, bf16[1152,768]{0,1:T(8,128)(2,1)S(1)} %copy-done.11), kind=kOutput, calls=%fused_computation.28 | convolution fusion | flops 3625451520 | bytes 9633792 | tf_op jit(solution)/shard_map/dot_general | solution.py:13
  355.9 8.3 %fusion.14 = bf16[1,2048,768]{2,1,0:T(8,128)(2,1)} fusion(bf16[1152,2048]{1,0:T(8,128)(2,1)} %reshape.207, bf16[1152,768]{0,1:T(8,128)(2,1)S(1)} %copy-done.15), kind=kOutput, calls=%fused_computation.29 | convolution fusion | flops 3625451520 | bytes 9633792 | tf_op jit(solution)/shard_map/dot_general | solution.py:13
  364.2 6.2 %fusion.15 = bf16[1,768,2048]{2,1,0:T(8,128)(2,1)} fusion(bf16[1152,2048]{1,0:T(8,128)(2,1)S(1)} %bitcast.51, f32[1152]{0:T(1024)S(1)} %reshape.211, f32[1152,768]{0,1:T(8,128)S(1)} %copy-done.13, f32[1152,768]{0,1:T(8,128)S(1)} %copy-done.12), kind=kOutput, calls=%fused_computation.30 | convolution fusion | flops 3637837824 | bytes 14946816 | tf_op jit(solution)/shard_map/dot_general | solution.py:13
  370.8 6.8 %gather_fusion.4 = bf16[1024]{0:T(1024)(128)(2,1)S(1)} fusion(bf16[1152]{0:T(1024)(128)(2,1)S(1)} %reshape.210, s32[1024]{0:T(1024)S(1)} %broadcast_clamp_fusion), kind=kCustom, calls=%fused_computation.4 | custom fusion | bytes 8192 | tf_op jit(solution)/shard_map/gather | solution.py:105
  379.8 66.4 %all-to-all-done.3 = bf16[128,9,2048]{2,1,0:T(8,128)(2,1)} async-done(((bf16[128,9,2048]{2,1,0:T(8,128)(2,1)}), bf16[128,9,2048]{2,1,0:T(8,128)(2,1)}, u32[]{:S(2)}, u32[]{:S(2)}) %all-to-all-start.3) | async-done | bytes 4718624 | tf_op jit(solution)/shard_map/all_to_all | solution.py:86
  446.2 8.5 %reshape.209 = bf16[1152,2048]{1,0:T(8,128)(2,1)} reshape(bf16[128,9,2048]{2,1,0:T(8,128)(2,1)} %all-to-all-done.3) | data formatting | bytes 9437184 | tf_op jit(solution)/shard_map/reshape | solution.py:101
  454.6 12.0 %gather_fusion.3 = bf16[1024,2048]{1,0:T(8,128)(2,1)} fusion(bf16[1152,2048]{1,0:T(8,128)(2,1)} %reshape.209, s32[1024]{0:T(1024)S(1)} %broadcast_clamp_fusion), kind=kCustom, calls=%fused_computation.3 | custom fusion | bytes 8392704 | tf_op jit(solution)/shard_map/gather | solution.py:101
  466.7 5.2 convert_reduce_fusion
  473.4 67.4 %psum.15 = f32[2048]{0:T(1024)} all-reduce(f32[2048]{0:T(1024)S(1)} %get-tuple-element.6), channel_id=1, replica_groups=mesh['dp'=8,'expert'=16] {'dp','expert'}, use_global_device_ids=true, to_apply=%region_15.16 | all-reduce | flops 2048 | bytes 16384 | tf_op jit(solution)/shard_map/psum | solution.py:113
  540.8 2.8 fusion.23
  543.6 25.3 %all-reduce.4.cloned.1.call-done = f32[2048,128]{1,0:T(8,128)} async-done(((f32[2048,128]{1,0:T(8,128)}), f32[2048,128]{1,0:T(8,128)}) %all-reduce.4.cloned.1.call-update) | async-done | bytes 1048592 | tf_op jit(solution)/shard_map/psum | solution.py:113
  (87 shorter events, 22.6 us)
Async XLA Ops:
  7.2 187.2 %copy-start = (bf16[1,2048,768]{2,1,0:T(8,128)(2,1)S(1)}, bf16[1,2048,768]{2,1,0:T(8,128)(2,1)}, u32[]{:S(2)}) copy-start(bf16[1,2048,768]{2,1,0:T(8,128)(2,1)} %param.13) | copy-start | bytes 9437188
  7.2 10.5 %copy-start.8 = (f32[2048]{0:T(1024)S(1)}, f32[2048]{0:T(1024)}, u32[]{:S(2)}) copy-start(f32[2048]{0:T(1024)} %param.9) | copy-start | bytes 24580
  10.9 0.8 copy-start.6
  18.9 0.8 copy-start.2
  30.1 33.3 %all-to-all-start = ((bf16[128,1,9]{2,1,0:T(2,128)(2,1)}), bf16[128,1,9]{2,1,0:T(2,128)(2,1)S(1)}, u32[]{:S(2)}, u32[]{:S(2)}) async-start(bf16[128,1,9]{2,1,0:T(2,128)(2,1)} %all_to_all.25), calls=%async_computation | async-start | bytes 131072 | tf_op jit(solution)/shard_map/all_to_all | solution.py:75
  63.4 107.8 %all-to-all-start.2 = ((bf16[128,9,2048]{2,1,0:T(8,128)(2,1)}), bf16[128,9,2048]{2,1,0:T(8,128)(2,1)}, u32[]{:S(2)}, u32[]{:S(2)}) async-start(bf16[128,9,2048]{2,1,0:T(8,128)(2,1)} %reshape.206), calls=%async_computation.2 | async-start | bytes 16777216 | tf_op jit(solution)/shard_map/all_to_all | solution.py:73
  171.3 111.6 %all-to-all-start.1 = ((bf16[128,9,2048]{2,1,0:T(8,128)(2,1)}), bf16[128,9,2048]{2,1,0:T(8,128)(2,1)}, u32[]{:S(2)}, u32[]{:S(2)}) async-start(bf16[128,9,2048]{2,1,0:T(8,128)(2,1)} %reshape.204), calls=%async_computation.1 | async-start | bytes 16777216 | tf_op jit(solution)/shard_map/all_to_all | solution.py:74
  194.4 8.5 %copy-start.5 = (bf16[1152,2048]{1,0:T(8,128)(2,1)S(1)}, bf16[1152,2048]{1,0:T(8,128)(2,1)}, u32[]{:S(2)}) copy-start(bf16[1152,2048]{1,0:T(8,128)(2,1)} %reshape.207) | copy-start | bytes 14155780
  194.4 8.5 %copy-start.9 = (bf16[1,2048,768]{2,1,0:T(8,128)(2,1)S(1)}, bf16[1,2048,768]{2,1,0:T(8,128)(2,1)}, u32[]{:S(2)}) copy-start(bf16[1,2048,768]{2,1,0:T(8,128)(2,1)} %param.14) | copy-start | bytes 9437188
  305.0 32.0 %all-to-all-start.4 = ((bf16[128,1,9]{2,1,0:T(2,128)(2,1)}), bf16[128,1,9]{2,1,0:T(2,128)(2,1)S(1)}, u32[]{:S(2)}, u32[]{:S(2)}) async-start(bf16[128,1,9]{2,1,0:T(2,128)(2,1)} %convert_element_type.122), calls=%async_computation.4 | async-start | bytes 131072 | tf_op jit(solution)/shard_map/all_to_all | solution.py:93
  317.6 5.6 copy-start.10
  317.6 5.6 copy-start.14
  337.1 10.3 %copy-start.11 = (bf16[1152,768]{0,1:T(8,128)(2,1)S(1)}, bf16[1152,768]{0,1:T(8,128)(2,1)}, u32[]{:S(2)}) copy-start(bf16[1152,768]{0,1:T(8,128)(2,1)} %get-tuple-element.9) | copy-start | bytes 5308420
  337.1 109.1 %all-to-all-start.3 = ((bf16[128,9,2048]{2,1,0:T(8,128)(2,1)}), bf16[128,9,2048]{2,1,0:T(8,128)(2,1)}, u32[]{:S(2)}, u32[]{:S(2)}) async-start(bf16[128,9,2048]{2,1,0:T(8,128)(2,1)} %reshape.208), calls=%async_computation.3 | async-start | bytes 16777216 | tf_op jit(solution)/shard_map/all_to_all | solution.py:86
  347.3 221.6 %all-reduce.4.cloned.1.call-start = ((), (), s32[]{:S(2)}) async-start(), calls=%async_computation.5 | async-start | bytes 2097152 | tf_op jit(solution)/shard_map/psum | solution.py:113
  347.4 8.5 %copy-start.15 = (bf16[1152,768]{0,1:T(8,128)(2,1)S(1)}, bf16[1152,768]{0,1:T(8,128)(2,1)}, u32[]{:S(2)}) copy-start(bf16[1152,768]{0,1:T(8,128)(2,1)} %get-tuple-element.10) | copy-start | bytes 5308420
  347.4 16.8 %slice-start = ((s8[4718592]{0:T(1024)(128)(4,1)}), s8[4194304]{0:T(1024)(128)(4,1)S(1)}, s32[]{:S(2)}) async-start(s8[4718592]{0:T(1024)(128)(4,1)} %bitcast.50), calls=%async_computation.6 | async-start | bytes 8388608
  355.9 8.3 %slice-start.1 = ((s8[4718592]{0:T(1024)(128)(4,1)}), s8[524288]{0:T(1024)(128)(4,1)S(1)}, s32[]{:S(2)}) async-start(s8[4718592]{0:T(1024)(128)(4,1)} %bitcast.50), calls=%async_computation.7 | async-start | bytes 1048576
  355.9 8.3 %copy-start.12 = (f32[1152,768]{0,1:T(8,128)S(1)}, f32[1152,768]{0,1:T(8,128)}, u32[]{:S(2)}) copy-start(f32[1152,768]{0,1:T(8,128)} %fusion.6) | copy-start | bytes 10616836
  355.9 8.3 %copy-start.13 = (f32[1152,768]{0,1:T(8,128)S(1)}, f32[1152,768]{0,1:T(8,128)}, u32[]{:S(2)}) copy-start(f32[1152,768]{0,1:T(8,128)} %fusion.9) | copy-start | bytes 10616836
  364.2 14.2 %copy-start.3 = (bf16[128,2048]{1,0:T(8,128)(2,1)S(1)}, bf16[128,2048]{1,0:T(8,128)(2,1)}, u32[]{:S(2)}) copy-start(bf16[128,2048]{1,0:T(8,128)(2,1)} %copy-done.2) | copy-start | bytes 1572868
  466.6 5.3 copy-start.4
  466.6 5.3 copy-start.7
  466.7 104.5 %copy-start.1 = (bf16[1,2048,768]{2,1,0:T(8,128)(2,1)S(1)}, bf16[1,2048,768]{2,1,0:T(8,128)(2,1)}, u32[]{:S(2)}) copy-start(bf16[1,2048,768]{2,1,0:T(8,128)(2,1)} %param.13) | copy-start | bytes 9437188
Sparse Core Ops, SparseCore 0:
  379.9 188.9 all-reduce.3
where the time goes:
time: 588 us; the launch traced here: 578 us
  waiting for transfers between devices  241 us (41%)
  local copies, waits for them, and re-layouts  115 us (20%)
  blocking collectives  67.4 us (11%)
  matrix products  65.8 us (11%)
  starting transfers between devices  58.8 us (10%)
  between operations  14.9 us (3%)
  other arithmetic  14.8 us (3%)
    all_to_all x1, waiting for transfers between devices, local(): lax.all_to_all(send_rows, ('dp', 'expert'), split_axis=0, concat_axis=0,...  75.9 us
    all_to_all x1, waiting for transfers between devices, local(): lax.all_to_all(send_grads, ('dp', 'expert'), split_axis=0, concat_axis=0,...  73.6 us
    psum x1, blocking collectives, local(): lax.psum((router_part, gain_part), ('dp', 'expert'))  67.4 us
    all_to_all x1, waiting for transfers between devices, local(): lax.all_to_all(grad_inputs.reshape(experts, capacity, model_width), ('dp'...  66.4 us
    dot_general x8, matrix products, contract(): lax.dot_general(left, right, (((left_dim,), (right_dim,)), ((), ())), pre...  49.6 us
    psum x1, waiting for transfers between devices, local(): lax.psum((router_part, gain_part), ('dp', 'expert'))  25.3 us
    all_to_all x1, starting transfers between devices, local(): lax.all_to_all(send_grads, ('dp', 'expert'), split_axis=0, concat_axis=0,...  14.3 us
    all_to_all x1, starting transfers between devices, local(): lax.all_to_all(route_grad.reshape(experts, capacity), ('dp', 'expert'), s...  12.6 us
  transfers between devices with their start and end apart: 6, of which 4 were waited for; matrix products, arithmetic and copies ran while one was open for 26% of the time, Pallas kernels for 0%

commit v1 on v0

v1 whole, which is shorter than its diff:
```python
import jax
import jax.numpy as jnp
from jax import lax
from jax.sharding import PartitionSpec as P


def silu_parts(value):
    sigmoid_v = jax.nn.sigmoid(value)
    return (value * sigmoid_v, sigmoid_v * (1.0 + value * (1.0 - sigmoid_v)))


def dims(left, right, left_dims, right_dims):
    return lax.dot_general(
        left, right, ((left_dims, right_dims), ((), ())), preferred_element_type=jnp.float32
    )


def expert_backward(rows_x, rows_y, prob_rows, gate_mat, up_mat, down_mat):
    slots, chunks, lanes = rows_x.shape
    ff = gate_mat.shape[1]
    gate3 = gate_mat.reshape(chunks, lanes, ff)
    up3 = up_mat.reshape(chunks, lanes, ff)
    down3 = down_mat.reshape(ff, chunks, lanes)
    pre_gate = dims(rows_x, gate3, (1, 2), (0, 1))
    pre_up = dims(rows_x, up3, (1, 2), (0, 1))
    activated, derivative = silu_parts(pre_gate)
    hidden_act = activated * pre_up
    grad_mid = dims(rows_y, down3, (1, 2), (1, 2))
    route_grad = jnp.sum(grad_mid * hidden_act, axis=1).astype(jnp.bfloat16)
    prob_col = prob_rows.astype(jnp.float32)[:, None]
    scaled = prob_col * grad_mid
    grad_pre_gate = (scaled * pre_up * derivative).astype(jnp.bfloat16)
    grad_pre_up = (scaled * activated).astype(jnp.bfloat16)
    scaled_up = (prob_col[:, :, None] * rows_y.astype(jnp.float32)).astype(jnp.bfloat16)
    grad_gate_mat = dims(rows_x, grad_pre_gate, (0,), (0,)).astype(jnp.bfloat16)
    grad_up_mat = dims(rows_x, grad_pre_up, (0,), (0,)).astype(jnp.bfloat16)
    grad_down_mat = dims(hidden_act.astype(jnp.bfloat16), scaled_up, (0,), (0,)).astype(jnp.bfloat16)
    grad_inputs = (
        dims(grad_pre_gate, gate3, (1,), (2,)) + dims(grad_pre_up, up3, (1,), (2,))
    ).astype(jnp.bfloat16)
    return (
        grad_gate_mat.reshape(chunks * lanes, ff),
        grad_up_mat.reshape(chunks * lanes, ff),
        grad_down_mat.reshape(ff, chunks * lanes),
        grad_inputs,
        route_grad,
    )


def local(
    hidden_in, norm_gain, router_weight, grad_out, expert_ids, gate_weight, up_weight, down_weight
):
    f32, bf16 = jnp.float32, jnp.bfloat16
    tok_rows, model_width = hidden_in.shape
    top_count = expert_ids.shape[1]
    experts = router_weight.shape[1]
    capacity = max(2, (tok_rows * top_count * 9 + 8 * experts - 1) // (8 * experts))
    slots = experts * capacity
    lanes = 128
    chunks = model_width // lanes
    axes = ("dp", "expert")

    values = hidden_in.astype(f32)
    inv_rms = lax.rsqrt(jnp.mean(values * values, axis=1, keepdims=True) + 1e-06)
    normed = (values * inv_rms * norm_gain).astype(bf16)
    logits = jnp.dot(normed, router_weight, preferred_element_type=f32)
    chosen = expert_ids[:, :, None] == jnp.arange(experts, dtype=jnp.int32)[None, None, :]
    picked = jnp.sum(jnp.where(chosen, logits[:, None, :], 0.0), axis=2)
    route_prob = jax.nn.softmax(picked, axis=1)
    prob_bf = route_prob.astype(bf16)

    flat_ids = expert_ids.reshape(-1)
    onehot = (flat_ids[:, None] == jnp.arange(experts, dtype=jnp.int32)[None, :]).astype(jnp.int32)
    counts = jnp.cumsum(onehot, axis=0)
    slot_idx = jnp.sum(counts * onehot, axis=1) - 1
    target = (flat_ids * capacity + slot_idx).reshape(tok_rows, top_count)
    hit = target[None, :, :] == jnp.arange(slots, dtype=jnp.int32)[:, None, None]
    sel_tok = jnp.any(hit, axis=2).astype(bf16)
    send_p = jnp.sum(jnp.where(hit, prob_bf.astype(f32)[None], 0.0), axis=(1, 2)).astype(bf16)

    normed3 = normed.reshape(tok_rows, chunks, lanes)
    grads3 = grad_out.reshape(tok_rows, chunks, lanes)
    send_x = dims(sel_tok, normed3, (1,), (0,)).astype(bf16).reshape(experts, capacity, chunks, lanes)
    send_y = dims(sel_tok, grads3, (1,), (0,)).astype(bf16).reshape(experts, capacity, chunks, lanes)
    recv_x = lax.all_to_all(send_x, axes, 0, 0, tiled=True)
    recv_y = lax.all_to_all(send_y, axes, 0, 0, tiled=True)
    recv_p = lax.all_to_all(send_p.reshape(experts, capacity), axes, 0, 0, tiled=True)

    grad_gate_mat, grad_up_mat, grad_down_mat, grad_inputs, route_grad = expert_backward(
        recv_x.reshape(slots, chunks, lanes),
        recv_y.reshape(slots, chunks, lanes),
        recv_p.reshape(slots),
        gate_weight[0],
        up_weight[0],
        down_weight[0],
    )
    back_inputs = lax.all_to_all(
        grad_inputs.reshape(experts, capacity, chunks, lanes), axes, 0, 0, tiled=True
    )
    back_grads = lax.all_to_all(route_grad.reshape(experts, capacity), axes, 0, 0, tiled=True)

    route_sum = dims(sel_tok, back_inputs.reshape(slots, chunks, lanes), (0,), (0,)).reshape(
        tok_rows, model_width
    )
    grad_prob = jnp.sum(
        jnp.where(hit, back_grads.reshape(slots).astype(f32)[:, None, None], 0.0), axis=0
    )
    grad_picked = route_prob * (grad_prob - jnp.sum(route_prob * grad_prob, axis=1, keepdims=True))
    grad_logit = jnp.sum(jnp.where(chosen, grad_picked[:, :, None], 0.0), axis=1).astype(bf16)
    router_part = dims(normed, grad_logit, (0,), (0,))
    grad_normed = route_sum + dims(grad_logit, router_weight, (1,), (1,))
    gain_part = jnp.sum(grad_normed * values * inv_rms, axis=0)
    packed = jnp.concatenate([router_part, gain_part.reshape(-1, experts)], axis=0)
    packed = lax.psum(packed, axes)
    grad_router = packed[:model_width]
    grad_gain = packed[model_width:].reshape(model_width)
    scaled = norm_gain * grad_normed
    cube = inv_rms * inv_rms * inv_rms
    grad_hidden = (
        grad_out.astype(f32)
        + inv_rms * scaled
        - values * cube * jnp.mean(scaled * values, axis=1, keepdims=True)
    ).astype(bf16)
    return (
        grad_hidden,
        grad_router,
        grad_gain,
        grad_gate_mat[None],
        grad_up_mat[None],
        grad_down_mat[None],
    )


def solution(mesh):
    in_specs = (
        P(("dp", "expert"), None),
        P(),
        P(),
        P(("dp", "expert"), None),
        P(("dp", "expert"), None),
        P(("dp", "expert"), None, None),
        P(("dp", "expert"), None, None),
        P(("dp", "expert"), None, None),
    )
    out_specs = (
        P(("dp", "expert"), None),
        P(),
        P(),
        P(("dp", "expert"), None, None),
        P(("dp", "expert"), None, None),
        P(("dp", "expert"), None, None),
    )
    return jax.shard_map(local, mesh=mesh, in_specs=in_specs, out_specs=out_specs, check_vma=False)
```

time: 588 us -> 487 us (0.83)
  blocking collectives: 67.4 us -> 13.9 us
  local copies, waits for them, and re-layouts: 115 us -> 81.2 us
  starting transfers between devices: 58.8 us -> 28.2 us
  other arithmetic: 14.8 us -> 35.9 us
  waiting for transfers between devices: 241 us -> 230 us
  matrix products: 65.8 us -> 73.3 us
    all_to_all x5 -> x4, waiting for transfers between devices: 216 us -> 87.4 us  [the longest x1 40.5 us: local(): recv_x = lax.all_to_all(send_x, axes, 0, 0, tiled=True)]
    psum x1, waiting for transfers between devices: 25.3 us -> 142 us  [local(): packed = lax.psum(packed, axes)]
    psum x1 -> x0, blocking collectives: 67.4 us -> none  [local(): lax.psum((router_part, gain_part), ('dp', 'expert'))]
    convert_element_type x2 -> x6, local copies, waits for them, and re-layouts: 0.18 us -> 50.2 us  [the longest x1 14.4 us: expert_backward(): grad_inputs = (dims(grad_pre_gate, gate3, (1,), (2,)) + dims(grad_pre_up,...]
    gather x5 -> x0, local copies, waits for them, and re-layouts: 49.7 us -> none  [the longest x1 12 us: local(): back_inputs.reshape(experts * capacity, model_width)[target]]
    reshape x7 -> x2, local copies, waits for them, and re-layouts: 50.1 us -> 8.76 us  [the longest x1 7.47 us: local(): recv_x.reshape(slots, chunks, lanes)]
    all_to_all x5 -> x4, starting transfers between devices: 58.8 us -> 28.2 us  [the longest x1 11.9 us: local(): recv_x = lax.all_to_all(send_x, axes, 0, 0, tiled=True)]
    all_to_all x0 -> x1, blocking collectives: none -> 13.9 us  [local(): lax.all_to_all(send_p.reshape(experts, capacity), axes, 0, 0, tiled=True)]
  transfers between devices with their start and end apart: 6 -> 5, of which waited for: 4 -> 5; matrix products, arithmetic and copies ran while one was open for 26% -> 20% of each run, Pallas kernels for 0% -> 0%
where the time goes in v1:
time: 487 us; the launch traced here: 477 us
  waiting for transfers between devices  230 us (47%)
  local copies, waits for them, and re-layouts  81.2 us (17%)
  matrix products  73.3 us (15%)
  other arithmetic  35.9 us (7%)
  starting transfers between devices  28.2 us (6%)
  between operations  14.8 us (3%)
  blocking collectives  13.9 us (3%)
    psum x1, waiting for transfers between devices, local(): packed = lax.psum(packed, axes)  142 us
    dot_general x12, matrix products, dims(): lax.dot_general(left, right, ((left_dims, right_dims), ((), ())), preferr...  63.4 us
    all_to_all x1, waiting for transfers between devices, local(): recv_x = lax.all_to_all(send_x, axes, 0, 0, tiled=True)  40.5 us
    all_to_all x1, waiting for transfers between devices, local(): recv_y = lax.all_to_all(send_y, axes, 0, 0, tiled=True)  29.3 us
    convert_element_type x1, local copies, waits for them, and re-layouts, expert_backward(): grad_inputs = (dims(grad_pre_gate, gate3, (1,), (2,)) + dims(grad_pre_up,...  14.4 us
    convert_element_type x1, local copies, waits for them, and re-layouts, local(): dims(sel_tok, grads3, (1,), (0,)).astype(bf16)  14.2 us
    convert_element_type x1, local copies, waits for them, and re-layouts, local(): dims(sel_tok, normed3, (1,), (0,)).astype(bf16)  14.1 us
    all_to_all x1, blocking collectives, local(): lax.all_to_all(send_p.reshape(experts, capacity), axes, 0, 0, tiled=True)  13.9 us
  transfers between devices with their start and end apart: 5, of which 5 were waited for; matrix products, arithmetic and copies ran while one was open for 20% of the time, Pallas kernels for 0%

profile of v1, /device:TPU:1, one launch (start us, length us, event | category | flops | bytes accessed | tf_op | source)
XLA Modules:
  0.0 477.2 jit_solution(14169409892969007504)
XLA Ops:
  11.2 4.2 fusion.2
  19.1 14.1 %copy.141 = bf16[1152,16,128]{2,1,0:T(8,128)(2,1)} copy(bf16[1152,16,128]{2,0,1:T(8,128)(2,1)S(1)} %convolution_convert_fusion) | data formatting | bytes 9437184 | tf_op jit(solution)/shard_map/convert_element_type | solution.py:83
  33.3 11.9 %all-to-all-start.2 = ((bf16[128,9,16,128]{3,2,1,0:T(8,128)(2,1)}), bf16[128,9,16,128]{3,2,1,0:T(8,128)(2,1)}, u32[]{:S(2)}, u32[]{:S(2)}) async-start(bf16[128,9,16,128]{3,2,1,0:T(8,128)(2,1)} %bitcast.85), calls=%async_computation.2 | async-start | bytes 9437184 | tf_op jit(solution)/shard_map/all_to_all | solution.py:85
  47.6 14.2 %copy.137 = bf16[1152,16,128]{2,1,0:T(8,128)(2,1)} copy(bf16[1152,16,128]{2,0,1:T(8,128)(2,1)S(1)} %convolution_convert_fusion.1) | data formatting | bytes 9437184 | tf_op jit(solution)/shard_map/convert_element_type | solution.py:84
  61.8 40.5 %all-to-all-done.2 = bf16[128,9,16,128]{3,2,1,0:T(8,128)(2,1)} async-done(((bf16[128,9,16,128]{3,2,1,0:T(8,128)(2,1)}), bf16[128,9,16,128]{3,2,1,0:T(8,128)(2,1)}, u32[]{:S(2)}, u32[]{:S(2)}) %all-to-all-start.2) | async-done | bytes 4718624 | tf_op jit(solution)/shard_map/all_to_all | solution.py:85
  102.3 5.5 %all-to-all-start.1 = ((bf16[128,9,16,128]{3,2,1,0:T(8,128)(2,1)}), bf16[128,9,16,128]{3,2,1,0:T(8,128)(2,1)}, u32[]{:S(2)}, u32[]{:S(2)}) async-start(bf16[128,9,16,128]{3,2,1,0:T(8,128)(2,1)} %bitcast.84), calls=%async_computation.1 | async-start | bytes 9437184 | tf_op jit(solution)/shard_map/all_to_all | solution.py:86
  107.9 4.7 copy.173
  113.5 7.5 %copy.152 = bf16[1152,16,128]{0,2,1:T(8,128)(2,1)} copy(bf16[1152,16,128]{2,1,0:T(8,128)(2,1)} %bitcast.8) | data formatting | bytes 9437184 | tf_op jit(solution)/shard_map/reshape | solution.py:90
  121.0 8.7 %convolution_bitcast_fusion = f32[1152,768]{0,1:T(8,128)} fusion(bf16[1152,16,128]{0,2,1:T(8,128)(2,1)} %copy.152, bf16[16,128,768]{2,1,0:T(8,128)(2,1)S(1)} %bitcast.81), kind=kOutput, calls=%fused_computation.11 | convolution fusion | flops 3623878656 | bytes 11403264 | tf_op jit(solution)/shard_map/dot_general | solution.py:13
  129.7 6.1 %convolution_bitcast_fusion.1 = f32[1152,768]{0,1:T(8,128)} fusion(bf16[1152,16,128]{0,2,1:T(8,128)(2,1)S(1)} %copy-done.4, bf16[16,128,768]{2,1,0:T(8,128)(2,1)S(1)} %bitcast.93), kind=kOutput, calls=%fused_computation.12 | convolution fusion | flops 3623878656 | bytes 11403264 | tf_op jit(solution)/shard_map/dot_general | solution.py:13
  135.8 29.3 %all-to-all-done.1 = bf16[128,9,16,128]{3,2,1,0:T(8,128)(2,1)} async-done(((bf16[128,9,16,128]{3,2,1,0:T(8,128)(2,1)}), bf16[128,9,16,128]{3,2,1,0:T(8,128)(2,1)}, u32[]{:S(2)}, u32[]{:S(2)}) %all-to-all-start.1) | async-done | bytes 4718624 | tf_op jit(solution)/shard_map/all_to_all | solution.py:86
  165.1 11.8 %multiply_reduce_fusion = (bf16[1152]{0:T(1024)(128)(2,1)S(1)}, f32[1152,768]{0,1:T(8,128)}) fusion(f32[1152,768]{0,1:T(8,128)} %convolution_bitcast_fusion.1, f32[1152,768]{0,1:T(8,128)} %convolution_bitcast_fusion, bf16[768,16,128]{2,1,0:T(8,128)(2,1)} %bitcast.91, bf16[1152,16,128]{2,1,0:T(8,128)(2,1)} %bitcast.5), kind=kOutput, calls=%fused_computation.13 | convolution fusion | flops 3630070784 | bytes 18483456 | tf_op jit(solution)/shard_map/dot_general | solution.py:13
  177.7 5.1 %all-to-all-start.4 = ((bf16[128,1,9]{2,1,0:T(2,128)(2,1)}), bf16[128,1,9]{2,1,0:T(2,128)(2,1)S(1)}, u32[]{:S(2)}, u32[]{:S(2)}) async-start(bf16[128,1,9]{2,1,0:T(2,128)(2,1)} %convert_element_type.150), calls=%async_computation.4 | async-start | bytes 131072 | tf_op jit(solution)/shard_map/all_to_all | solution.py:100
  182.8 9.5 %all-to-all-done.4 = bf16[128,1,9]{2,1,0:T(2,128)(2,1)S(1)} async-done(((bf16[128,1,9]{2,1,0:T(2,128)(2,1)}), bf16[128,1,9]{2,1,0:T(2,128)(2,1)S(1)}, u32[]{:S(2)}, u32[]{:S(2)}) %all-to-all-start.4) | async-done | bytes 2336 | tf_op jit(solution)/shard_map/all_to_all | solution.py:100
  192.8 9.5 %select_reduce_fusion = (f32[128,8]{0,1:T(8,128)S(1)}, bf16[1152]{0:T(1024)(128)(2,1)S(1)}) fusion(f32[1152]{0:T(1024)S(1)} %reshape.237, s32[128,8]{0,1:T(8,128)S(1)} %multiply_add_fusion, f32[128,8]{0,1:T(8,128)S(1)} %convert_convert_fusion), kind=kLoop, calls=%fused_computation.6 | loop fusion | flops 5896064 | bytes 19200 | tf_op jit(solution)/shard_map/reduce_sum | solution.py:105
  202.5 13.9 %all_to_all.27 = bf16[128,1,9]{2,1,0:T(2,128)(2,1)S(1)} all-to-all(bf16[128,1,9]{2,1,0:T(2,128)(2,1)S(1)} %convert_element_type.149), channel_id=1, replica_groups=mesh['dp'=8,'expert'=16] {'dp','expert'}, dimensions={0} | all-to-all | bytes 4608 | tf_op jit(solution)/shard_map/all_to_all | solution.py:87
  216.8 5.0 %fusion.8 = (bf16[1152,768,1]{0,1,2:T(8,128)(2,1)S(1)}, bf16[1152,768]{0,1:T(8,128)(2,1)S(1)}) fusion(f32[1152,768]{0,1:T(8,128)} %get-tuple-element.45, f32[1152]{0:T(1024)S(1)} %reshape.236, f32[1152,768]{0,1:T(8,128)} %convolution_bitcast_fusion, f32[1152,768]{0,1:T(8,128)} %convolution_bitcast_fusion.1), kind=kLoop, calls=%fused_computation.27 | loop fusion | flops 12386304 | bytes 14160384 | tf_op jit(solution)/shard_map/convert_element_type | solution.py:33
  221.8 3.9 fusion.10
  225.7 4.2 add_convert_fusion
  230.0 14.4 %copy.148 = bf16[1152,16,128]{2,1,0:T(8,128)(2,1)} copy(bf16[1152,16,128]{2,0,1:T(8,128)(2,1)S(1)} %add_convert_fusion) | data formatting | bytes 9437184 | tf_op jit(solution)/shard_map/convert_element_type | solution.py:40
  244.3 5.6 %all-to-all-start.3 = ((bf16[128,9,16,128]{3,2,1,0:T(8,128)(2,1)}), bf16[128,9,16,128]{3,2,1,0:T(8,128)(2,1)}, u32[]{:S(2)}, u32[]{:S(2)}) async-start(bf16[128,9,16,128]{3,2,1,0:T(8,128)(2,1)} %bitcast.83), calls=%async_computation.3 | async-start | bytes 9437184 | tf_op jit(solution)/shard_map/all_to_all | solution.py:97
  251.9 7.0 %multiply_convert_fusion = bf16[1152,16,128]{2,1,0:T(8,128)(2,1)} fusion(f32[1152]{0:T(1024)S(1)} %reshape.236, bf16[128,9,16,128]{3,2,1,0:T(8,128)(2,1)} %all-to-all-done.1), kind=kLoop, calls=%fused_computation | loop fusion | flops 7077888 | bytes 9441792 | tf_op jit(solution)/shard_map/convert_element_type | solution.py:34
  258.9 7.1 %copy.157 = bf16[1152,16,128]{0,2,1:T(8,128)(2,1)} copy(bf16[1152,16,128]{2,1,0:T(8,128)(2,1)} %multiply_convert_fusion) | data formatting | bytes 9437184 | tf_op jit(solution)/shard_map/convert_element_type | solution.py:34
  266.0 9.6 %fusion.12 = f32[768,2048]{0,1:S(1)} fusion(bf16[1152,2048]{0,1:T(8,128)(2,1)} %bitcast.89, f32[1152,768]{0,1:T(8,128)} %convolution_bitcast_fusion.1, f32[1152,768]{0,1:T(8,128)} %convolution_bitcast_fusion), kind=kOutput, calls=%fused_computation.31 | convolution fusion | flops 3629187072 | bytes 18087936
  277.6 4.6 copy.158
  282.2 9.0 %convolution_convert_fusion.3 = bf16[16,128,768]{2,1,0:T(8,128)(2,1)} fusion(bf16[1152,16,128]{0,2,1:T(8,128)(2,1)} %copy.152, bf16[1152,768]{0,1:T(8,128)(2,1)} %copy-done.9), kind=kOutput, calls=%fused_computation.21 | convolution fusion | flops 3625451520 | bytes 9633792 | tf_op jit(solution)/shard_map/dot_general | solution.py:13
  291.2 8.0 %convolution_convert_fusion.2 = bf16[16,128,768]{2,1,0:T(8,128)(2,1)} fusion(bf16[1152,16,128]{0,2,1:T(8,128)(2,1)} %copy.152, bf16[1152,768,1]{0,1,2:T(8,128)(2,1)S(1)} %copy-done.8), kind=kOutput, calls=%fused_computation.20 | convolution fusion | flops 3625451520 | bytes 9633792 | tf_op jit(solution)/shard_map/dot_general | solution.py:13
  299.2 8.1 %all-to-all-done.3 = bf16[128,9,16,128]{3,2,1,0:T(8,128)(2,1)} async-done(((bf16[128,9,16,128]{3,2,1,0:T(8,128)(2,1)}), bf16[128,9,16,128]{3,2,1,0:T(8,128)(2,1)}, u32[]{:S(2)}, u32[]{:S(2)}) %all-to-all-start.3) | async-done | bytes 4718624 | tf_op jit(solution)/shard_map/all_to_all | solution.py:97
  307.3 7.1 %copy.149 = bf16[16,128,1152]{2,1,0:T(8,128)(2,1)} copy(bf16[16,128,1152]{1,0,2:T(8,128)(2,1)} %bitcast.17) | data formatting | bytes 9437184 | tf_op jit(solution)/shard_map/dot_general | solution.py:13
  314.3 4.1 fusion.33
  321.0 2.9 fusion.20
  323.9 142.4 %all-reduce.2.cloned.1.call-done = f32[2064,128]{1,0:T(8,128)} async-done(((f32[2064,128]{1,0:T(8,128)}), f32[2064,128]{1,0:T(8,128)}) %all-reduce.2.cloned.1.call-update) | async-done | bytes 1056784 | tf_op jit(solution)/shard_map/psum | solution.py:114
  (76 shorter events, 23.1 us)
Async XLA Ops:
  7.2 113.8 %copy-start = (bf16[1,2048,768]{2,1,0:T(8,128)(2,1)S(1)}, bf16[1,2048,768]{2,1,0:T(8,128)(2,1)}, u32[]{:S(2)}) copy-start(bf16[1,2048,768]{2,1,0:T(8,128)(2,1)} %param.13) | copy-start | bytes 9437188
  7.2 4.0 copy-start.13
  7.2 9.4 %copy-start.12 = (f32[2048]{0:T(1024)S(1)}, f32[2048]{0:T(1024)}, u32[]{:S(2)}) copy-start(f32[2048]{0:T(1024)} %param.9) | copy-start | bytes 24580
  8.6 0.8 copy-start.6
  33.3 69.1 %all-to-all-start.2 = ((bf16[128,9,16,128]{3,2,1,0:T(8,128)(2,1)}), bf16[128,9,16,128]{3,2,1,0:T(8,128)(2,1)}, u32[]{:S(2)}, u32[]{:S(2)}) async-start(bf16[128,9,16,128]{3,2,1,0:T(8,128)(2,1)} %bitcast.85), calls=%async_computation.2 | async-start | bytes 9437184 | tf_op jit(solution)/shard_map/all_to_all | solution.py:85
  102.3 62.7 %all-to-all-start.1 = ((bf16[128,9,16,128]{3,2,1,0:T(8,128)(2,1)}), bf16[128,9,16,128]{3,2,1,0:T(8,128)(2,1)}, u32[]{:S(2)}, u32[]{:S(2)}) async-start(bf16[128,9,16,128]{3,2,1,0:T(8,128)(2,1)} %bitcast.84), calls=%async_computation.1 | async-start | bytes 9437184 | tf_op jit(solution)/shard_map/all_to_all | solution.py:86
  107.9 4.7 copy-start.2
  107.9 4.7 copy-start.10
  121.0 8.7 %copy-start.4 = (bf16[1152,16,128]{0,2,1:T(8,128)(2,1)S(1)}, bf16[1152,16,128]{0,2,1:T(8,128)(2,1)}, u32[]{:S(2)}) copy-start(bf16[1152,16,128]{0,2,1:T(8,128)(2,1)} %copy.152) | copy-start | bytes 14155780
  121.0 8.7 %copy-start.14 = (bf16[1,2048,768]{2,1,0:T(8,128)(2,1)S(1)}, bf16[1,2048,768]{2,1,0:T(8,128)(2,1)}, u32[]{:S(2)}) copy-start(bf16[1,2048,768]{2,1,0:T(8,128)(2,1)} %param.14) | copy-start | bytes 9437188
  177.7 14.7 %all-to-all-start.4 = ((bf16[128,1,9]{2,1,0:T(2,128)(2,1)}), bf16[128,1,9]{2,1,0:T(2,128)(2,1)S(1)}, u32[]{:S(2)}, u32[]{:S(2)}) async-start(bf16[128,1,9]{2,1,0:T(2,128)(2,1)} %convert_element_type.150), calls=%async_computation.4 | async-start | bytes 131072 | tf_op jit(solution)/shard_map/all_to_all | solution.py:100
  221.8 3.9 copy-start.9
  221.8 3.9 copy-start.7
  221.8 3.9 copy-start.15
  244.3 6.2 %copy-start.3 = (bf16[128,2048]{1,0:T(8,128)(2,1)S(1)}, bf16[128,2048]{1,0:T(8,128)(2,1)}, u32[]{:S(2)}) copy-start(bf16[128,2048]{1,0:T(8,128)(2,1)} %param.8) | copy-start | bytes 1572868
  244.3 62.9 %all-to-all-start.3 = ((bf16[128,9,16,128]{3,2,1,0:T(8,128)(2,1)}), bf16[128,9,16,128]{3,2,1,0:T(8,128)(2,1)}, u32[]{:S(2)}, u32[]{:S(2)}) async-start(bf16[128,9,16,128]{3,2,1,0:T(8,128)(2,1)} %bitcast.83), calls=%async_computation.3 | async-start | bytes 9437184 | tf_op jit(solution)/shard_map/all_to_all | solution.py:97
  249.9 216.4 %all-reduce.2.cloned.1.call-start = ((), (), s32[]{:S(2)}) async-start(), calls=%async_computation.5 | async-start | bytes 2113536 | tf_op jit(solution)/shard_map/psum | solution.py:114
  282.2 9.0 %copy-start.8 = (bf16[1152,768,1]{0,1,2:T(8,128)(2,1)S(1)}, bf16[1152,768,1]{0,1,2:T(8,128)(2,1)}, u32[]{:S(2)}) copy-start(bf16[1152,768,1]{0,1,2:T(8,128)(2,1)} %copy-done.7) | copy-start | bytes 5308420
  314.3 4.1 copy-start.11
  314.3 5.5 %copy-start.5 = (f32[2048,128]{1,0:T(8,128)S(1)}, f32[2048,128]{1,0:T(8,128)}, u32[]{:S(2)}) copy-start(f32[2048,128]{1,0:T(8,128)} %fusion.36) | copy-start | bytes 3145732
  319.9 150.0 %copy-start.1 = (bf16[1,2048,768]{2,1,0:T(8,128)(2,1)S(1)}, bf16[1,2048,768]{2,1,0:T(8,128)(2,1)}, u32[]{:S(2)}) copy-start(bf16[1,2048,768]{2,1,0:T(8,128)(2,1)} %param.13) | copy-start | bytes 9437188
Sparse Core Ops, SparseCore 0:
  321.1 145.1 all-reduce.1

commit v2 on v1

--- a/solution.py
+++ b/solution.py
@@ -102,18 +102,23 @@
     route_sum = dims(sel_tok, back_inputs.reshape(slots, chunks, lanes), (0,), (0,)).reshape(
         tok_rows, model_width
     )
-    grad_prob = jnp.sum(
-        jnp.where(hit, back_grads.reshape(slots).astype(f32)[:, None, None], 0.0), axis=0
-    )
+    grad_prob = back_grads.reshape(slots)[target].astype(f32)
     grad_picked = route_prob * (grad_prob - jnp.sum(route_prob * grad_prob, axis=1, keepdims=True))
     grad_logit = jnp.sum(jnp.where(chosen, grad_picked[:, :, None], 0.0), axis=1).astype(bf16)
     router_part = dims(normed, grad_logit, (0,), (0,))
     grad_normed = route_sum + dims(grad_logit, router_weight, (1,), (1,))
     gain_part = jnp.sum(grad_normed * values * inv_rms, axis=0)
-    packed = jnp.concatenate([router_part, gain_part.reshape(-1, experts)], axis=0)
-    packed = lax.psum(packed, axes)
-    grad_router = packed[:model_width]
-    grad_gain = packed[model_width:].reshape(model_width)
+    n_dev = experts
+    rows_per = model_width // n_dev
+    gain_per = model_width // n_dev
+    gain_rows = jnp.pad(gain_part.reshape(n_dev, 1, gain_per), ((0, 0), (0, 0), (0, experts - gain_per)))
+    send_sum = jnp.concatenate([router_part.reshape(n_dev, rows_per, experts), gain_rows], axis=1)
+    part_sum = jnp.sum(lax.all_to_all(send_sum, axes, 0, 0, tiled=True), axis=0)
+    whole = lax.all_to_all(
+        jnp.broadcast_to(part_sum[None], (n_dev,) + part_sum.shape), axes, 0, 0, tiled=True
+    )
+    grad_router = whole[:, :rows_per, :].reshape(model_width, experts)
+    grad_gain = whole[:, rows_per, :gain_per].reshape(model_width)
     scaled = norm_gain * grad_normed
     cube = inv_rms * inv_rms * inv_rms
     grad_hidden = (

time: 487 us -> 377 us (0.77)
  waiting for transfers between devices: 230 us -> 115 us
  starting transfers between devices: 28.2 us -> 55 us
  blocking collectives: 13.9 us -> 0 us
  between operations: 14.8 us -> 1.25 us
  local copies, waits for them, and re-layouts: 81.2 us -> 90.7 us
  other arithmetic: 35.9 us -> 30 us
  matrix products: 73.3 us -> 78.5 us
    psum x1 -> x0, waiting for transfers between devices: 142 us -> none  [local(): packed = lax.psum(packed, axes)]
    all_to_all x0 -> x3, starting transfers between devices: none -> 23.1 us  [the longest x1 11.8 us: local(): lax.all_to_all(send_p.reshape(experts, capacity), axes, 0, 0, tiled=True)]
    all_to_all x1, waiting for transfers between devices: 8.06 us -> 26.6 us  [local(): lax.all_to_all(grad_inputs.reshape(experts, capacity, chunks, lanes), axe...]
    all_to_all x0 -> x3, waiting for transfers between devices: none -> 17.9 us  [the longest x1 12.6 us: local(): part_sum = jnp.sum(lax.all_to_all(send_sum, axes, 0, 0, tiled=True), axis=0)]
    all_to_all x1 -> x0, blocking collectives: 13.9 us -> none  [local(): lax.all_to_all(send_p.reshape(experts, capacity), axes, 0, 0, tiled=True)]
    all_to_all x1, waiting for transfers between devices: 9.52 us -> 0.01 us  [local(): lax.all_to_all(route_grad.reshape(experts, capacity), axes, 0, 0, tiled=T...]
    gather x0 -> x1, local copies, waits for them, and re-layouts: none -> 6.8 us  [local(): grad_prob = back_grads.reshape(slots)[target].astype(f32)]
    convert_element_type x2 -> x0, other arithmetic: 5.18 us -> none  [the longest x1 4.99 us: expert_backward(): grad_pre_up = (scaled * activated).astype(jnp.bfloat16)]
  transfers between devices with their start and end apart: 5 -> 7, of which waited for: 5 -> 5; matrix products, arithmetic and copies ran while one was open for 20% -> 40% of each run, Pallas kernels for 0% -> 0%
where the time goes in v2:
time: 377 us; the launch traced here: 371 us
  waiting for transfers between devices  115 us (31%)
  local copies, waits for them, and re-layouts  90.7 us (24%)
  matrix products  78.5 us (21%)
  starting transfers between devices  55 us (15%)
  other arithmetic  30 us (8%)
    dot_general x12, matrix products, dims(): lax.dot_general(left, right, ((left_dims, right_dims), ((), ())), preferr...  65.5 us
    all_to_all x1, waiting for transfers between devices, local(): recv_x = lax.all_to_all(send_x, axes, 0, 0, tiled=True)  40.4 us
    all_to_all x1, waiting for transfers between devices, local(): recv_y = lax.all_to_all(send_y, axes, 0, 0, tiled=True)  30.2 us
    all_to_all x1, waiting for transfers between devices, local(): lax.all_to_all(grad_inputs.reshape(experts, capacity, chunks, lanes), axe...  26.6 us
    convert_element_type x1, local copies, waits for them, and re-layouts, expert_backward(): grad_inputs = (dims(grad_pre_gate, gate3, (1,), (2,)) + dims(grad_pre_up,...  14.2 us
    convert_element_type x1, local copies, waits for them, and re-layouts, local(): dims(sel_tok, grads3, (1,), (0,)).astype(bf16)  14.1 us
    convert_element_type x1, local copies, waits for them, and re-layouts, local(): dims(sel_tok, normed3, (1,), (0,)).astype(bf16)  14.1 us
    all_to_all x1, waiting for transfers between devices, local(): part_sum = jnp.sum(lax.all_to_all(send_sum, axes, 0, 0, tiled=True), axis=0)  12.6 us
  transfers between devices with their start and end apart: 7, of which 5 were waited for; matrix products, arithmetic and copies ran while one was open for 40% of the time, Pallas kernels for 0%

profile of v2, /device:TPU:1, one launch (start us, length us, event | category | flops | bytes accessed | tf_op | source)
XLA Modules:
  0.0 370.5 jit_solution(13845056242497431778)
XLA Ops:
  8.1 8.7 %select_reduce_fusion = bf16[1152]{0:T(1024)(128)(2,1)S(1)} fusion(f32[128,8]{0,1:T(8,128)S(1)} %convert_convert_fusion, s32[128,8]{0,1:T(8,128)S(1)} %get-tuple-element.39), kind=kLoop, calls=%fused_computation.7 | loop fusion | flops 3537792 | bytes 10496 | tf_op jit(solution)/shard_map/reduce_sum | solution.py:79
  17.6 11.8 %all-to-all-start = ((bf16[128,1,9]{2,1,0:T(2,128)(2,1)}), bf16[128,1,9]{2,1,0:T(2,128)(2,1)S(1)}, u32[]{:S(2)}, u32[]{:S(2)}) async-start(bf16[128,1,9]{2,1,0:T(2,128)(2,1)} %convert_element_type.147), calls=%async_computation | async-start | bytes 131072 | tf_op jit(solution)/shard_map/all_to_all | solution.py:87
  29.4 4.2 %fusion.2 = pred[1152,128]{1,0:T(8,128)(4,1)S(1)} fusion(s32[128,8]{0,1:T(8,128)S(1)} %get-tuple-element.39), kind=kLoop, calls=%fused_computation.9 | loop fusion | flops 2211840 | bytes 151552 | tf_op jit(solution)/shard_map/reduce_or | solution.py:78
  36.1 14.1 %copy.137 = bf16[1152,16,128]{2,1,0:T(8,128)(2,1)} copy(bf16[1152,16,128]{2,0,1:T(8,128)(2,1)S(1)} %convolution_convert_fusion) | data formatting | bytes 9437184 | tf_op jit(solution)/shard_map/convert_element_type | solution.py:83
  50.3 10.7 %all-to-all-start.2 = ((bf16[128,9,16,128]{3,2,1,0:T(8,128)(2,1)}), bf16[128,9,16,128]{3,2,1,0:T(8,128)(2,1)}, u32[]{:S(2)}, u32[]{:S(2)}) async-start(bf16[128,9,16,128]{3,2,1,0:T(8,128)(2,1)} %bitcast.87), calls=%async_computation.2 | async-start | bytes 9437184 | tf_op jit(solution)/shard_map/all_to_all | solution.py:85
  63.4 14.1 %copy.133 = bf16[1152,16,128]{2,1,0:T(8,128)(2,1)} copy(bf16[1152,16,128]{2,0,1:T(8,128)(2,1)S(1)} %convolution_convert_fusion.1) | data formatting | bytes 9437184 | tf_op jit(solution)/shard_map/convert_element_type | solution.py:84
  77.6 40.4 %all-to-all-done.2 = bf16[128,9,16,128]{3,2,1,0:T(8,128)(2,1)} async-done(((bf16[128,9,16,128]{3,2,1,0:T(8,128)(2,1)}), bf16[128,9,16,128]{3,2,1,0:T(8,128)(2,1)}, u32[]{:S(2)}, u32[]{:S(2)}) %all-to-all-start.2) | async-done | bytes 4718624 | tf_op jit(solution)/shard_map/all_to_all | solution.py:85
  118.0 5.5 %all-to-all-start.1 = ((bf16[128,9,16,128]{3,2,1,0:T(8,128)(2,1)}), bf16[128,9,16,128]{3,2,1,0:T(8,128)(2,1)}, u32[]{:S(2)}, u32[]{:S(2)}) async-start(bf16[128,9,16,128]{3,2,1,0:T(8,128)(2,1)} %bitcast.86), calls=%async_computation.1 | async-start | bytes 9437184 | tf_op jit(solution)/shard_map/all_to_all | solution.py:86
  123.5 4.6 %copy.172 = bf16[96,8,16,128]{3,2,1,0:T(8,128)(2,1)} copy(bf16[96,8,16,128]{3,1,2,0:T(8,128)(2,1)} %bitcast.93) | data formatting | bytes 6291456
  128.5 7.2 %copy.152 = bf16[1152,16,128]{0,2,1:T(8,128)(2,1)} copy(bf16[1152,16,128]{2,1,0:T(8,128)(2,1)} %bitcast.8) | data formatting | bytes 9437184 | tf_op jit(solution)/shard_map/reshape | solution.py:90
  135.8 8.6 %convolution_bitcast_fusion = f32[1152,768]{0,1:T(8,128)} fusion(bf16[1152,16,128]{0,2,1:T(8,128)(2,1)} %copy.152, bf16[16,128,768]{2,1,0:T(8,128)(2,1)S(1)} %bitcast.83), kind=kOutput, calls=%fused_computation.11 | convolution fusion | flops 3623878656 | bytes 11403264 | tf_op jit(solution)/shard_map/dot_general | solution.py:13
  144.4 6.1 %convolution_bitcast_fusion.1 = f32[1152,768]{0,1:T(8,128)} fusion(bf16[1152,16,128]{0,2,1:T(8,128)(2,1)S(1)} %copy-done.4, bf16[16,128,768]{2,1,0:T(8,128)(2,1)S(1)} %bitcast.97), kind=kOutput, calls=%fused_computation.12 | convolution fusion | flops 3623878656 | bytes 11403264 | tf_op jit(solution)/shard_map/dot_general | solution.py:13
  150.5 30.2 %all-to-all-done.1 = bf16[128,9,16,128]{3,2,1,0:T(8,128)(2,1)} async-done(((bf16[128,9,16,128]{3,2,1,0:T(8,128)(2,1)}), bf16[128,9,16,128]{3,2,1,0:T(8,128)(2,1)}, u32[]{:S(2)}, u32[]{:S(2)}) %all-to-all-start.1) | async-done | bytes 4718624 | tf_op jit(solution)/shard_map/all_to_all | solution.py:86
  180.7 13.2 %multiply_reduce_fusion = (bf16[1152]{0:T(1024)(128)(2,1)S(1)}, bf16[1152,768]{0,1:T(8,128)(2,1)}, bf16[1152,768,1]{0,1,2:T(8,128)(2,1)}) fusion(f32[1152,768]{0,1:T(8,128)} %convolution_bitcast_fusion.1, f32[1152,768]{0,1:T(8,128)} %convolution_bitcast_fusion, f32[1152]{0:T(1024)S(1)} %reshape.240, bf16[768,16,128]{2,1,0:T(8,128)(2,1)} %bitcast.94, ...), kind=kOutput, calls=%fused_computation.13 | convolution fusion | flops 3638918144 | bytes 18488064 | tf_op jit(solution)/shard_map/dot_general | solution.py:13
  194.8 5.1 %all-to-all-start.4 = ((bf16[128,1,9]{2,1,0:T(2,128)(2,1)}), bf16[128,1,9]{2,1,0:T(2,128)(2,1)S(1)}, u32[]{:S(2)}, u32[]{:S(2)}) async-start(bf16[128,1,9]{2,1,0:T(2,128)(2,1)} %convert_element_type.148), calls=%async_computation.4 | async-start | bytes 131072 | tf_op jit(solution)/shard_map/all_to_all | solution.py:100
  199.9 5.5 %fusion.10 = f32[1152,16,128]{2,0,1:T(8,128)S(1)} fusion(bf16[16,128,768]{2,1,0:T(8,128)(2,1)S(1)} %bitcast.84, bf16[1152,768]{0,1:T(8,128)(2,1)} %get-tuple-element.41), kind=kOutput, calls=%fused_computation.29 | convolution fusion | flops 3623878656 | bytes 14352384 | tf_op jit(solution)/shard_map/dot_general | solution.py:13
  205.5 4.2 %add_convert_fusion = bf16[1152,16,128]{2,0,1:T(8,128)(2,1)S(1)} fusion(f32[1152,16,128]{2,0,1:T(8,128)S(1)} %fusion.10, bf16[1152,768,1]{0,1,2:T(8,128)(2,1)S(1)} %copy-done.12, bf16[16,128,768]{2,1,0:T(8,128)(2,1)S(1)} %bitcast.98), kind=kOutput, calls=%fused_computation.2 | convolution fusion | flops 3628597248 | bytes 19070976 | tf_op jit(solution)/shard_map/dot_general | solution.py:13
  209.7 14.2 %copy.144 = bf16[1152,16,128]{2,1,0:T(8,128)(2,1)} copy(bf16[1152,16,128]{2,0,1:T(8,128)(2,1)S(1)} %add_convert_fusion) | data formatting | bytes 9437184 | tf_op jit(solution)/shard_map/convert_element_type | solution.py:40
  223.9 10.5 %all-to-all-start.3 = ((bf16[128,9,16,128]{3,2,1,0:T(8,128)(2,1)}), bf16[128,9,16,128]{3,2,1,0:T(8,128)(2,1)}, u32[]{:S(2)}, u32[]{:S(2)}) async-start(bf16[128,9,16,128]{3,2,1,0:T(8,128)(2,1)} %bitcast.85), calls=%async_computation.3 | async-start | bytes 9437184 | tf_op jit(solution)/shard_map/all_to_all | solution.py:97
  234.6 6.7 %multiply_convert_fusion = bf16[1152,16,128]{2,1,0:T(8,128)(2,1)} fusion(f32[1152]{0:T(1024)S(1)} %reshape.240, bf16[128,9,16,128]{3,2,1,0:T(8,128)(2,1)} %all-to-all-done.1), kind=kLoop, calls=%fused_computation.1 | loop fusion | flops 7077888 | bytes 9441792 | tf_op jit(solution)/shard_map/convert_element_type | solution.py:34
  241.3 7.2 %copy.157 = bf16[1152,16,128]{0,2,1:T(8,128)(2,1)} copy(bf16[1152,16,128]{2,1,0:T(8,128)(2,1)} %multiply_convert_fusion) | data formatting | bytes 9437184 | tf_op jit(solution)/shard_map/convert_element_type | solution.py:34
  248.5 8.0 %convolution_convert_fusion.3 = bf16[16,128,768]{2,1,0:T(8,128)(2,1)} fusion(bf16[1152,16,128]{0,2,1:T(8,128)(2,1)} %copy.152, bf16[1152,768]{0,1:T(8,128)(2,1)S(1)} %copy-done.11), kind=kOutput, calls=%fused_computation.21 | convolution fusion | flops 3625451520 | bytes 9633792 | tf_op jit(solution)/shard_map/dot_general | solution.py:13
  256.9 6.8 %gather_fusion = bf16[1024]{0:T(1024)(128)(2,1)S(1)} fusion(bf16[1152]{0:T(1024)(128)(2,1)S(1)} %reshape.236, s32[1024]{0:T(1024)S(1)} %broadcast_clamp_fusion), kind=kCustom, calls=%fused_computation | custom fusion | bytes 8192 | tf_op jit(solution)/shard_map/gather | solution.py:105
  264.8 26.6 %all-to-all-done.3 = bf16[128,9,16,128]{3,2,1,0:T(8,128)(2,1)} async-done(((bf16[128,9,16,128]{3,2,1,0:T(8,128)(2,1)}), bf16[128,9,16,128]{3,2,1,0:T(8,128)(2,1)}, u32[]{:S(2)}, u32[]{:S(2)}) %all-to-all-start.3) | async-done | bytes 4718624 | tf_op jit(solution)/shard_map/all_to_all | solution.py:97
  291.4 7.1 %copy.145 = bf16[16,128,1152]{2,1,0:T(8,128)(2,1)} copy(bf16[16,128,1152]{1,0,2:T(8,128)(2,1)} %bitcast.17) | data formatting | bytes 9437184 | tf_op jit(solution)/shard_map/dot_general | solution.py:13
  305.4 5.1 %all-to-all-start.5 = ((f32[128,17,128]{2,1,0:T(8,128)}), f32[128,17,128]{2,1,0:T(8,128)S(1)}, u32[]{:S(2)}, u32[]{:S(2)}) async-start(f32[128,17,128]{2,1,0:T(8,128)} %pad_maximum_fusion), calls=%async_computation.5 | async-start | bytes 3145728 | tf_op jit(solution)/shard_map/all_to_all | solution.py:116
  310.5 11.4 %fusion.12 = f32[768,2048]{0,1} fusion(bf16[1152,2048]{0,1:T(8,128)(2,1)} %bitcast.91, f32[1152,768]{0,1:T(8,128)} %convolution_bitcast_fusion.1, f32[1152,768]{0,1:T(8,128)} %convolution_bitcast_fusion), kind=kOutput, calls=%fused_computation.31 | convolution fusion | flops 3629187072 | bytes 18087936
  321.9 12.6 %all-to-all-done.5 = f32[128,17,128]{2,1,0:T(8,128)S(1)} async-done(((f32[128,17,128]{2,1,0:T(8,128)}), f32[128,17,128]{2,1,0:T(8,128)S(1)}, u32[]{:S(2)}, u32[]{:S(2)}) %all-to-all-start.5) | async-done | bytes 1114144 | tf_op jit(solution)/shard_map/all_to_all | solution.py:116
  336.1 6.1 %all-to-all-start.6 = ((f32[128,17,128]{2,1,0:T(8,128)}), f32[128,17,128]{2,1,0:T(8,128)}, u32[]{:S(2)}, u32[]{:S(2)}) async-start(f32[128,17,128]{2,1,0:T(8,128)} %broadcast_in_dim.64), calls=%async_computation.6 | async-start | bytes 3145728 | tf_op jit(solution)/shard_map/all_to_all | solution.py:117
  342.2 9.0 %convolution_convert_fusion.2 = bf16[16,128,768]{2,1,0:T(8,128)(2,1)} fusion(bf16[1152,16,128]{0,2,1:T(8,128)(2,1)} %copy.152, bf16[1152,768,1]{0,1,2:T(8,128)(2,1)} %get-tuple-element.42), kind=kOutput, calls=%fused_computation.20 | convolution fusion | flops 3625451520 | bytes 9633792 | tf_op jit(solution)/shard_map/dot_general | solution.py:13
  353.3 4.8 %copy.158 = bf16[1,768,2048]{2,1,0:T(8,128)(2,1)} copy(bf16[1,768,2048]{1,2,0:T(8,128)(2,1)} %bitcast.89) | data formatting | bytes 6291456
  360.8 5.3 %all-to-all-done.6 = f32[128,17,128]{2,1,0:T(8,128)} async-done(((f32[128,17,128]{2,1,0:T(8,128)}), f32[128,17,128]{2,1,0:T(8,128)}, u32[]{:S(2)}, u32[]{:S(2)}) %all-to-all-start.6) | async-done | bytes 1114144 | tf_op jit(solution)/shard_map/all_to_all | solution.py:117
  (82 shorter events, 33.4 us)
Async XLA Ops:
  0.6 135.1 %copy-start = (bf16[1,2048,768]{2,1,0:T(8,128)(2,1)S(1)}, bf16[1,2048,768]{2,1,0:T(8,128)(2,1)}, u32[]{:S(2)}) copy-start(bf16[1,2048,768]{2,1,0:T(8,128)(2,1)} %param.13) | copy-start | bytes 9437188
  0.6 7.4 %copy-start.8 = (s32[128,8]{0,1:T(8,128)S(1)}, s32[128,8]{0,1:T(8,128)}, u32[]{:S(2)}) copy-start(s32[128,8]{0,1:T(8,128)} %param.12) | copy-start | bytes 12292
  0.7 33.0 %copy-start.7 = (f32[2048]{0:T(1024)S(1)}, f32[2048]{0:T(1024)}, u32[]{:S(2)}) copy-start(f32[2048]{0:T(1024)} %param.9) | copy-start | bytes 24580
  5.5 0.8 copy-start.5
  17.6 32.6 %all-to-all-start = ((bf16[128,1,9]{2,1,0:T(2,128)(2,1)}), bf16[128,1,9]{2,1,0:T(2,128)(2,1)S(1)}, u32[]{:S(2)}, u32[]{:S(2)}) async-start(bf16[128,1,9]{2,1,0:T(2,128)(2,1)} %convert_element_type.147), calls=%async_computation | async-start | bytes 131072 | tf_op jit(solution)/shard_map/all_to_all | solution.py:87
  50.3 67.7 %all-to-all-start.2 = ((bf16[128,9,16,128]{3,2,1,0:T(8,128)(2,1)}), bf16[128,9,16,128]{3,2,1,0:T(8,128)(2,1)}, u32[]{:S(2)}, u32[]{:S(2)}) async-start(bf16[128,9,16,128]{3,2,1,0:T(8,128)(2,1)} %bitcast.87), calls=%async_computation.2 | async-start | bytes 9437184 | tf_op jit(solution)/shard_map/all_to_all | solution.py:85
  118.0 62.7 %all-to-all-start.1 = ((bf16[128,9,16,128]{3,2,1,0:T(8,128)(2,1)}), bf16[128,9,16,128]{3,2,1,0:T(8,128)(2,1)}, u32[]{:S(2)}, u32[]{:S(2)}) async-start(bf16[128,9,16,128]{3,2,1,0:T(8,128)(2,1)} %bitcast.86), calls=%async_computation.1 | async-start | bytes 9437184 | tf_op jit(solution)/shard_map/all_to_all | solution.py:86
  135.8 8.6 %copy-start.4 = (bf16[1152,16,128]{0,2,1:T(8,128)(2,1)S(1)}, bf16[1152,16,128]{0,2,1:T(8,128)(2,1)}, u32[]{:S(2)}) copy-start(bf16[1152,16,128]{0,2,1:T(8,128)(2,1)} %copy.152) | copy-start | bytes 14155780
  135.8 8.6 %copy-start.9 = (bf16[1,2048,768]{2,1,0:T(8,128)(2,1)S(1)}, bf16[1,2048,768]{2,1,0:T(8,128)(2,1)}, u32[]{:S(2)}) copy-start(bf16[1,2048,768]{2,1,0:T(8,128)(2,1)} %param.14) | copy-start | bytes 9437188
  194.8 29.1 %all-to-all-start.4 = ((bf16[128,1,9]{2,1,0:T(2,128)(2,1)}), bf16[128,1,9]{2,1,0:T(2,128)(2,1)S(1)}, u32[]{:S(2)}, u32[]{:S(2)}) async-start(bf16[128,1,9]{2,1,0:T(2,128)(2,1)} %convert_element_type.148), calls=%async_computation.4 | async-start | bytes 131072 | tf_op jit(solution)/shard_map/all_to_all | solution.py:100
  199.9 5.6 %copy-start.10 = (bf16[1,2048,768]{2,1,0:T(8,128)(2,1)S(1)}, bf16[1,2048,768]{2,1,0:T(8,128)(2,1)}, u32[]{:S(2)}) copy-start(bf16[1,2048,768]{2,1,0:T(8,128)(2,1)} %param.14) | copy-start | bytes 9437188
  199.9 5.6 %copy-start.12 = (bf16[1152,768,1]{0,1,2:T(8,128)(2,1)S(1)}, bf16[1152,768,1]{0,1,2:T(8,128)(2,1)}, u32[]{:S(2)}) copy-start(bf16[1152,768,1]{0,1,2:T(8,128)(2,1)} %get-tuple-element.42) | copy-start | bytes 5308420
  223.9 67.5 %all-to-all-start.3 = ((bf16[128,9,16,128]{3,2,1,0:T(8,128)(2,1)}), bf16[128,9,16,128]{3,2,1,0:T(8,128)(2,1)}, u32[]{:S(2)}, u32[]{:S(2)}) async-start(bf16[128,9,16,128]{3,2,1,0:T(8,128)(2,1)} %bitcast.85), calls=%async_computation.3 | async-start | bytes 9437184 | tf_op jit(solution)/shard_map/all_to_all | solution.py:97
  241.3 7.2 %copy-start.11 = (bf16[1152,768]{0,1:T(8,128)(2,1)S(1)}, bf16[1152,768]{0,1:T(8,128)(2,1)}, u32[]{:S(2)}) copy-start(bf16[1152,768]{0,1:T(8,128)(2,1)} %get-tuple-element.41) | copy-start | bytes 5308420
  256.9 7.5 %copy-start.2 = (bf16[128,2048]{1,0:T(8,128)(2,1)S(1)}, bf16[128,2048]{1,0:T(8,128)(2,1)}, u32[]{:S(2)}) copy-start(bf16[128,2048]{1,0:T(8,128)(2,1)} %param.8) | copy-start | bytes 1572868
  298.5 4.0 %copy-start.6 = (bf16[2048,128]{1,0:T(8,128)(2,1)S(1)}, bf16[2048,128]{1,0:T(8,128)(2,1)}, u32[]{:S(2)}) copy-start(bf16[2048,128]{1,0:T(8,128)(2,1)} %param.10) | copy-start | bytes 1572868
  305.4 29.2 %all-to-all-start.5 = ((f32[128,17,128]{2,1,0:T(8,128)}), f32[128,17,128]{2,1,0:T(8,128)S(1)}, u32[]{:S(2)}, u32[]{:S(2)}) async-start(f32[128,17,128]{2,1,0:T(8,128)} %pad_maximum_fusion), calls=%async_computation.5 | async-start | bytes 3145728 | tf_op jit(solution)/shard_map/all_to_all | solution.py:116
  336.1 30.0 %all-to-all-start.6 = ((f32[128,17,128]{2,1,0:T(8,128)}), f32[128,17,128]{2,1,0:T(8,128)}, u32[]{:S(2)}, u32[]{:S(2)}) async-start(f32[128,17,128]{2,1,0:T(8,128)} %broadcast_in_dim.64), calls=%async_computation.6 | async-start | bytes 3145728 | tf_op jit(solution)/shard_map/all_to_all | solution.py:117
  342.2 9.0 %copy-start.3 = (f32[768,2048]{0,1:S(1)}, f32[768,2048]{0,1}, u32[]{:S(2)}) copy-start(f32[768,2048]{0,1} %fusion.12) | copy-start | bytes 18874372
  353.3 17.0 %copy-start.1 = (bf16[1,2048,768]{2,1,0:T(8,128)(2,1)S(1)}, bf16[1,2048,768]{2,1,0:T(8,128)(2,1)}, u32[]{:S(2)}) copy-start(bf16[1,2048,768]{2,1,0:T(8,128)(2,1)} %param.13) | copy-start | bytes 9437188

commit v3 on v2

--- a/solution.py
+++ b/solution.py
@@ -56,6 +56,7 @@
     experts = router_weight.shape[1]
     capacity = max(2, (tok_rows * top_count * 9 + 8 * experts - 1) // (8 * experts))
     slots = experts * capacity
+    routes = tok_rows * top_count
     lanes = 128
     chunks = model_width // lanes
     axes = ("dp", "expert")
@@ -74,21 +75,30 @@
     counts = jnp.cumsum(onehot, axis=0)
     slot_idx = jnp.sum(counts * onehot, axis=1) - 1
     target = (flat_ids * capacity + slot_idx).reshape(tok_rows, top_count)
-    hit = target[None, :, :] == jnp.arange(slots, dtype=jnp.int32)[:, None, None]
-    sel_tok = jnp.any(hit, axis=2).astype(bf16)
-    send_p = jnp.sum(jnp.where(hit, prob_bf.astype(f32)[None], 0.0), axis=(1, 2)).astype(bf16)
+    owner = (
+        jnp.full((slots,), routes, jnp.int32)
+        .at[target.reshape(-1)]
+        .set(jnp.arange(routes, dtype=jnp.int32))
+    )
+    token_of = jnp.minimum(owner // top_count, tok_rows)
+    pad_probs = jnp.concatenate([prob_bf.reshape(-1), jnp.zeros((1,), bf16)], axis=0)
+    send_p = pad_probs[owner]
 
-    normed3 = normed.reshape(tok_rows, chunks, lanes)
-    grads3 = grad_out.reshape(tok_rows, chunks, lanes)
-    send_x = dims(sel_tok, normed3, (1,), (0,)).astype(bf16).reshape(experts, capacity, chunks, lanes)
-    send_y = dims(sel_tok, grads3, (1,), (0,)).astype(bf16).reshape(experts, capacity, chunks, lanes)
-    recv_x = lax.all_to_all(send_x, axes, 0, 0, tiled=True)
-    recv_y = lax.all_to_all(send_y, axes, 0, 0, tiled=True)
+    both3 = jnp.concatenate(
+        [
+            normed.reshape(tok_rows, chunks, lanes),
+            grad_out.reshape(tok_rows, chunks, lanes),
+        ],
+        axis=1,
+    )
+    both3 = jnp.concatenate([both3, jnp.zeros((1, 2 * chunks, lanes), bf16)], axis=0)
+    send_xy = both3[token_of].reshape(experts, capacity, 2 * chunks, lanes)
+    recv_xy = lax.all_to_all(send_xy, axes, 0, 0, tiled=True).reshape(slots, 2 * chunks, lanes)
     recv_p = lax.all_to_all(send_p.reshape(experts, capacity), axes, 0, 0, tiled=True)
 
     grad_gate_mat, grad_up_mat, grad_down_mat, grad_inputs, route_grad = expert_backward(
-        recv_x.reshape(slots, chunks, lanes),
-        recv_y.reshape(slots, chunks, lanes),
+        recv_xy[:, :chunks],
+        recv_xy[:, chunks:],
         recv_p.reshape(slots),
         gate_weight[0],
         up_weight[0],
@@ -99,9 +109,8 @@
     )
     back_grads = lax.all_to_all(route_grad.reshape(experts, capacity), axes, 0, 0, tiled=True)
 
-    route_sum = dims(sel_tok, back_inputs.reshape(slots, chunks, lanes), (0,), (0,)).reshape(
-        tok_rows, model_width
-    )
+    back3 = back_inputs.reshape(slots, chunks, lanes)
+    route_sum = jnp.sum(back3[target].astype(f32), axis=1).reshape(tok_rows, model_width)
     grad_prob = back_grads.reshape(slots)[target].astype(f32)
     grad_picked = route_prob * (grad_prob - jnp.sum(route_prob * grad_prob, axis=1, keepdims=True))
     grad_logit = jnp.sum(jnp.where(chosen, grad_picked[:, :, None], 0.0), axis=1).astype(bf16)

time: 377 us -> 389 us (1.032)
  waiting for transfers between devices: 115 us -> 149 us
  matrix products: 78.5 us -> 60.8 us
  starting transfers between devices: 55 us -> 63 us
  other arithmetic: 30 us -> 23 us
  local copies, waits for them, and re-layouts: 90.7 us -> 83.9 us
    all_to_all x2 -> x1, waiting for transfers between devices: 70.6 us -> 106 us  [local(): lax.all_to_all(send_xy, axes, 0, 0, tiled=True)]
    convert_element_type x3 -> x1, local copies, waits for them, and re-layouts: 29.1 us -> 0.1 us  [local(): prob_bf = route_prob.astype(bf16)]
    gather x0 -> x3, local copies, waits for them, and re-layouts: none -> 25.3 us  [the longest x1 10.8 us: local(): back3[target].astype(f32)]
    dot_general x12 -> x9, matrix products: 65.5 us -> 47.8 us  [dims(): lax.dot_general(left, right, ((left_dims, right_dims), ((), ())), preferr...]
    all_to_all x1, starting transfers between devices: 5.12 us -> 19.4 us  [local(): lax.all_to_all(route_grad.reshape(experts, capacity), axes, 0, 0, tiled=T...]
    reshape x1 -> x0, local copies, waits for them, and re-layouts: 7.24 us -> none  [local(): recv_x.reshape(slots, chunks, lanes)]
    dot_general x1 -> x0, local copies, waits for them, and re-layouts: 7.08 us -> none  [dims(): lax.dot_general(left, right, ((left_dims, right_dims), ((), ())), preferr...]
    all_to_all x2 -> x1, starting transfers between devices: 16.3 us -> 10.2 us  [local(): lax.all_to_all(send_xy, axes, 0, 0, tiled=True)]
  transfers between devices with their start and end apart: 7 -> 6, of which waited for: 5 -> 4; matrix products, arithmetic and copies ran while one was open for 40% -> 27% of each run, Pallas kernels for 0% -> 0%
where the time goes in v3:
time: 389 us; the launch traced here: 382 us
  waiting for transfers between devices  149 us (38%)
  local copies, waits for them, and re-layouts  83.9 us (22%)
  starting transfers between devices  63 us (16%)
  matrix products  60.8 us (16%)
  other arithmetic  23 us (6%)
    all_to_all x1, waiting for transfers between devices, local(): lax.all_to_all(send_xy, axes, 0, 0, tiled=True)  106 us
    dot_general x9, matrix products, dims(): lax.dot_general(left, right, ((left_dims, right_dims), ((), ())), preferr...  47.8 us
    all_to_all x1, waiting for transfers between devices, local(): lax.all_to_all(grad_inputs.reshape(experts, capacity, chunks, lanes), axe...  26 us
    all_to_all x1, starting transfers between devices, local(): lax.all_to_all(route_grad.reshape(experts, capacity), axes, 0, 0, tiled=T...  19.4 us
    convert_element_type x1, local copies, waits for them, and re-layouts, expert_backward(): grad_inputs = (dims(grad_pre_gate, gate3, (1,), (2,)) + dims(grad_pre_up,...  14.4 us
    all_to_all x1, waiting for transfers between devices, local(): part_sum = jnp.sum(lax.all_to_all(send_sum, axes, 0, 0, tiled=True), axis=0)  12.5 us
    unnamed x37, local copies, waits for them, and re-layouts  12.4 us
    all_to_all x1, starting transfers between devices, local(): lax.all_to_all(send_p.reshape(experts, capacity), axes, 0, 0, tiled=True)  11.5 us
  transfers between devices with their start and end apart: 6, of which 4 were waited for; matrix products, arithmetic and copies ran while one was open for 27% of the time, Pallas kernels for 0%

profile of v3, /device:TPU:1, one launch (start us, length us, event | category | flops | bytes accessed | tf_op | source)
XLA Modules:
  0.0 381.6 jit_solution(3284864122094310976)
XLA Ops:
  8.5 4.3 %scatter_custom_fusion = s32[1152]{0:T(1024)S(1)} fusion(s32[1024]{0:T(1024)S(1)} %bitcast.84, s32[1024]{0:T(1024)S(1)} %iota.15, s32[]{:T(128)} %constant.23.clone.1), kind=kCustom, calls=%fused_computation.92 | custom fusion | bytes 4612 | tf_op jit(solution)/shard_map/scatter | solution.py:81
  12.8 7.3 %gather_fusion = bf16[1152]{0:T(1024)(128)(2,1)S(1)} fusion(bf16[1025]{0:T(1024)(128)(2,1)S(1)} %pad_maximum_fusion.1, s32[2048]{0:T(1024)S(1)} %get-tuple-element.45), kind=kCustom, calls=%fused_computation | custom fusion | bytes 9216 | tf_op jit(solution)/shard_map/gather | solution.py:85
  21.0 11.5 %all-to-all-start = ((bf16[128,1,9]{2,1,0:T(2,128)(2,1)}), bf16[128,1,9]{2,1,0:T(2,128)(2,1)S(1)}, u32[]{:S(2)}, u32[]{:S(2)}) async-start(bf16[128,1,9]{2,1,0:T(2,128)(2,1)} %all_to_all.29), calls=%async_computation | async-start | bytes 131072 | tf_op jit(solution)/shard_map/all_to_all | solution.py:97
  36.2 7.3 %gather_fusion.1 = bf16[1152,32,128]{2,1,0:T(8,128)(2,1)} fusion(bf16[129,32,128]{2,1,0:T(8,128)(2,1)} %fusion.28, s32[2048]{0:T(1024)S(1)} %get-tuple-element.44), kind=kCustom, calls=%fused_computation.1 | custom fusion | bytes 18878976 | tf_op jit(solution)/shard_map/gather | solution.py:95
  43.4 10.2 %all-to-all-start.1 = ((bf16[128,9,32,128]{3,2,1,0:T(8,128)(2,1)}), bf16[128,9,32,128]{3,2,1,0:T(8,128)(2,1)}, u32[]{:S(2)}, u32[]{:S(2)}) async-start(bf16[128,9,32,128]{3,2,1,0:T(8,128)(2,1)} %bitcast.69), calls=%async_computation.1 | async-start | bytes 18874368 | tf_op jit(solution)/shard_map/all_to_all | solution.py:96
  53.6 4.6 %copy.116 = bf16[96,8,16,128]{3,2,1,0:T(8,128)(2,1)} copy(bf16[96,8,16,128]{3,1,2,0:T(8,128)(2,1)} %bitcast.76) | data formatting | bytes 6291456
  58.6 105.9 %all-to-all-done.1 = bf16[128,9,32,128]{3,2,1,0:T(8,128)(2,1)} async-done(((bf16[128,9,32,128]{3,2,1,0:T(8,128)(2,1)}), bf16[128,9,32,128]{3,2,1,0:T(8,128)(2,1)}, u32[]{:S(2)}, u32[]{:S(2)}) %all-to-all-start.1) | async-done | bytes 9437216 | tf_op jit(solution)/shard_map/all_to_all | solution.py:96
  164.4 5.1 %fusion.58 = (bf16[1152,16,128]{2,1,0:T(8,128)(2,1)S(1)}, bf16[1152,16,128]{2,1,0:T(8,128)(2,1)S(1)}) fusion(bf16[1152,32,128]{2,1,0:T(8,128)(2,1)} %bitcast.6), kind=kLoop, calls=%fused_computation.102 | loop fusion | bytes 18874368 | tf_op jit(solution)/shard_map/slice | solution.py:101
  169.6 4.6 %convolution_bitcast_fusion = f32[1152,768]{0,1:T(8,128)S(1)} fusion(bf16[16,128,768]{2,1,0:T(8,128)(2,1)S(1)} %bitcast.67, bf16[1152,16,128]{2,1,0:T(8,128)(2,1)S(1)} %get-tuple-element.35), kind=kOutput, calls=%fused_computation.11 | convolution fusion | flops 3623878656 | bytes 11403264 | tf_op jit(solution)/shard_map/dot_general | solution.py:13
  174.2 4.7 %convolution_bitcast_fusion.1 = f32[1152,768]{0,1:T(8,128)S(1)} fusion(bf16[16,128,768]{2,1,0:T(8,128)(2,1)S(1)} %bitcast.85, bf16[1152,16,128]{2,1,0:T(8,128)(2,1)S(1)} %get-tuple-element.35), kind=kOutput, calls=%fused_computation.12 | convolution fusion | flops 3623878656 | bytes 11403264 | tf_op jit(solution)/shard_map/dot_general | solution.py:13
  178.9 7.8 %multiply_reduce_fusion = (bf16[1152]{0:T(1024)(128)(2,1)S(1)}, bf16[1152,768]{0,1:T(8,128)(2,1)}, bf16[1152,768,1]{0,1,2:T(8,128)(2,1)}) fusion(f32[1152,768]{0,1:T(8,128)S(1)} %convolution_bitcast_fusion.1, f32[1152,768]{0,1:T(8,128)S(1)} %convolution_bitcast_fusion, f32[1152]{0:T(1024)S(1)} %reshape.230, bf16[768,16,128]{2,1,0:T(8,128)(2,1)S(1)} %bitcast.77, ...), kind=kOutput, calls=%fused_computation.13 | convolution fusion | flops 3638918144 | bytes 18488064 | tf_op jit(solution)/shard_map/dot_general | solution.py:13
  187.7 19.4 %all-to-all-start.3 = ((bf16[128,1,9]{2,1,0:T(2,128)(2,1)}), bf16[128,1,9]{2,1,0:T(2,128)(2,1)S(1)}, u32[]{:S(2)}, u32[]{:S(2)}) async-start(bf16[128,1,9]{2,1,0:T(2,128)(2,1)} %convert_element_type.120), calls=%async_computation.3 | async-start | bytes 131072 | tf_op jit(solution)/shard_map/all_to_all | solution.py:110
  207.1 5.5 %fusion.23 = f32[1152,16,128]{2,0,1:T(8,128)S(1)} fusion(bf16[16,128,768]{2,1,0:T(8,128)(2,1)S(1)} %bitcast.68, bf16[1152,768]{0,1:T(8,128)(2,1)} %get-tuple-element.33), kind=kOutput, calls=%fused_computation.38 | convolution fusion | flops 3623878656 | bytes 14352384 | tf_op jit(solution)/shard_map/dot_general | solution.py:13
  212.6 4.2 %add_convert_fusion = bf16[1152,16,128]{2,0,1:T(8,128)(2,1)S(1)} fusion(f32[1152,16,128]{2,0,1:T(8,128)S(1)} %fusion.23, bf16[1152,768,1]{0,1,2:T(8,128)(2,1)S(1)} %copy-done.15, bf16[16,128,768]{2,1,0:T(8,128)(2,1)S(1)} %bitcast.86), kind=kOutput, calls=%fused_computation.6 | convolution fusion | flops 3628597248 | bytes 19070976 | tf_op jit(solution)/shard_map/dot_general | solution.py:13
  216.8 14.4 %copy.89 = bf16[1152,16,128]{2,1,0:T(8,128)(2,1)} copy(bf16[1152,16,128]{2,0,1:T(8,128)(2,1)S(1)} %add_convert_fusion) | data formatting | bytes 9437184 | tf_op jit(solution)/shard_map/convert_element_type | solution.py:40
  231.3 10.6 %all-to-all-start.2 = ((bf16[128,9,16,128]{3,2,1,0:T(8,128)(2,1)}), bf16[128,9,16,128]{3,2,1,0:T(8,128)(2,1)}, u32[]{:S(2)}, u32[]{:S(2)}) async-start(bf16[128,9,16,128]{3,2,1,0:T(8,128)(2,1)} %bitcast.70), calls=%async_computation.2 | async-start | bytes 9437184 | tf_op jit(solution)/shard_map/all_to_all | solution.py:107
  242.0 6.1 %multiply_convert_fusion = bf16[1152,16,128]{2,0,1:T(8,128)(2,1)} fusion(f32[1152]{0:T(1024)S(1)} %reshape.230, bf16[1152,16,128]{2,1,0:T(8,128)(2,1)} %copy-done.2), kind=kLoop, calls=%fused_computation.5 | loop fusion | flops 7077888 | bytes 9441792 | tf_op jit(solution)/shard_map/convert_element_type | solution.py:34
  248.0 6.9 %copy.97 = bf16[1152,16,128]{0,2,1:T(8,128)(2,1)} copy(bf16[1152,16,128]{2,0,1:T(8,128)(2,1)} %multiply_convert_fusion) | data formatting | bytes 9437184 | tf_op jit(solution)/shard_map/convert_element_type | solution.py:34
  254.9 9.4 %fusion.13 = bf16[16,128,768]{2,1,0:T(8,128)(2,1)} fusion(bf16[1152,16,128]{2,1,0:T(8,128)(2,1)} %copy-done.5, bf16[1152,768]{0,1:T(8,128)(2,1)S(1)} %copy-done.12), kind=kOutput, calls=%fused_computation.26 | convolution fusion | flops 3625451520 | bytes 9633792 | tf_op jit(solution)/shard_map/dot_general | solution.py:13
  264.8 6.8 %gather_fusion.3 = bf16[1024]{0:T(1024)(128)(2,1)S(1)} fusion(bf16[1152]{0:T(1024)(128)(2,1)S(1)} %reshape.226, s32[1024]{0:T(1024)S(1)} %broadcast_clamp_fusion), kind=kCustom, calls=%fused_computation.3 | custom fusion | bytes 8192 | tf_op jit(solution)/shard_map/gather | solution.py:114
  272.8 26.0 %all-to-all-done.2 = bf16[128,9,16,128]{3,2,1,0:T(8,128)(2,1)} async-done(((bf16[128,9,16,128]{3,2,1,0:T(8,128)(2,1)}), bf16[128,9,16,128]{3,2,1,0:T(8,128)(2,1)}, u32[]{:S(2)}, u32[]{:S(2)}) %all-to-all-start.2) | async-done | bytes 4718624 | tf_op jit(solution)/shard_map/all_to_all | solution.py:107
  298.8 10.8 %gather_fusion.2 = bf16[1024,16,128]{2,1,0:T(8,128)(2,1)} fusion(bf16[1152,16,128]{2,1,0:T(8,128)(2,1)} %bitcast.15, s32[1024]{0:T(1024)S(1)} %broadcast_clamp_fusion), kind=kCustom, calls=%fused_computation.2 | custom fusion | bytes 8392704 | tf_op jit(solution)/shard_map/gather | solution.py:113
  309.6 3.5 convert_reduce_fusion
  316.2 5.5 %all-to-all-start.4 = ((f32[128,17,128]{2,1,0:T(8,128)}), f32[128,17,128]{2,1,0:T(8,128)S(1)}, u32[]{:S(2)}, u32[]{:S(2)}) async-start(f32[128,17,128]{2,1,0:T(8,128)} %pad_maximum_fusion), calls=%async_computation.4 | async-start | bytes 3145728 | tf_op jit(solution)/shard_map/all_to_all | solution.py:125
  321.7 11.4 %fusion.25 = f32[768,2048]{0,1} fusion(bf16[1152,2048]{0,1:T(8,128)(2,1)} %bitcast.73, f32[1152,768]{0,1:T(8,128)} %copy-done.14, f32[1152,768]{0,1:T(8,128)} %copy-done.13), kind=kOutput, calls=%fused_computation.40 | convolution fusion | flops 3629187072 | bytes 18087936
  333.1 12.5 %all-to-all-done.4 = f32[128,17,128]{2,1,0:T(8,128)S(1)} async-done(((f32[128,17,128]{2,1,0:T(8,128)}), f32[128,17,128]{2,1,0:T(8,128)S(1)}, u32[]{:S(2)}, u32[]{:S(2)}) %all-to-all-start.4) | async-done | bytes 1114144 | tf_op jit(solution)/shard_map/all_to_all | solution.py:125
  347.2 5.9 %all-to-all-start.5 = ((f32[128,17,128]{2,1,0:T(8,128)}), f32[128,17,128]{2,1,0:T(8,128)}, u32[]{:S(2)}, u32[]{:S(2)}) async-start(f32[128,17,128]{2,1,0:T(8,128)} %broadcast_in_dim.39), calls=%async_computation.5 | async-start | bytes 3145728 | tf_op jit(solution)/shard_map/all_to_all | solution.py:126
  353.1 9.4 %fusion.16 = bf16[16,128,768]{2,1,0:T(8,128)(2,1)} fusion(bf16[1152,768,1]{0,1,2:T(8,128)(2,1)} %get-tuple-element.36, bf16[1152,16,128]{2,1,0:T(8,128)(2,1)} %copy-done.5), kind=kOutput, calls=%fused_computation.27 | convolution fusion | flops 3625451520 | bytes 9633792 | tf_op jit(solution)/shard_map/dot_general | solution.py:13
  364.6 4.8 %copy.98 = bf16[1,768,2048]{2,1,0:T(8,128)(2,1)} copy(bf16[1,768,2048]{1,2,0:T(8,128)(2,1)} %bitcast.71) | data formatting | bytes 6291456
  369.4 2.8 fusion.34
  372.1 4.8 %all-to-all-done.5 = f32[128,17,128]{2,1,0:T(8,128)} async-done(((f32[128,17,128]{2,1,0:T(8,128)}), f32[128,17,128]{2,1,0:T(8,128)}, u32[]{:S(2)}, u32[]{:S(2)}) %all-to-all-start.5) | async-done | bytes 1114144 | tf_op jit(solution)/shard_map/all_to_all | solution.py:126
  378.9 2.3 slice.36
  (89 shorter events, 23.7 us)
Async XLA Ops:
  0.6 168.9 %copy-start = (bf16[1,2048,768]{2,1,0:T(8,128)(2,1)S(1)}, bf16[1,2048,768]{2,1,0:T(8,128)(2,1)}, u32[]{:S(2)}) copy-start(bf16[1,2048,768]{2,1,0:T(8,128)(2,1)} %param.13) | copy-start | bytes 9437188
  5.8 0.8 copy-start.7
  6.6 25.8 %copy-start.9 = (f32[2048]{0:T(1024)S(1)}, f32[2048]{0:T(1024)}, u32[]{:S(2)}) copy-start(f32[2048]{0:T(1024)} %param.9) | copy-start | bytes 24580
  21.0 22.5 %all-to-all-start = ((bf16[128,1,9]{2,1,0:T(2,128)(2,1)}), bf16[128,1,9]{2,1,0:T(2,128)(2,1)S(1)}, u32[]{:S(2)}, u32[]{:S(2)}) async-start(bf16[128,1,9]{2,1,0:T(2,128)(2,1)} %all_to_all.29), calls=%async_computation | async-start | bytes 131072 | tf_op jit(solution)/shard_map/all_to_all | solution.py:97
  43.4 121.0 %all-to-all-start.1 = ((bf16[128,9,32,128]{3,2,1,0:T(8,128)(2,1)}), bf16[128,9,32,128]{3,2,1,0:T(8,128)(2,1)}, u32[]{:S(2)}, u32[]{:S(2)}) async-start(bf16[128,9,32,128]{3,2,1,0:T(8,128)(2,1)} %bitcast.69), calls=%async_computation.1 | async-start | bytes 18874368 | tf_op jit(solution)/shard_map/all_to_all | solution.py:96
  169.5 4.7 %copy-start.5 = (bf16[1152,16,128]{2,1,0:T(8,128)(2,1)}, bf16[1152,16,128]{2,1,0:T(8,128)(2,1)S(1)}, u32[]{:S(2)}) copy-start(bf16[1152,16,128]{2,1,0:T(8,128)(2,1)S(1)} %get-tuple-element.35) | copy-start | bytes 14155780
  169.5 9.4 %copy-start.2 = (bf16[1152,16,128]{2,1,0:T(8,128)(2,1)}, bf16[1152,16,128]{2,1,0:T(8,128)(2,1)S(1)}, u32[]{:S(2)}) copy-start(bf16[1152,16,128]{2,1,0:T(8,128)(2,1)S(1)} %get-tuple-element.34) | copy-start | bytes 14155780
  169.5 4.7 %copy-start.10 = (bf16[1,2048,768]{2,1,0:T(8,128)(2,1)S(1)}, bf16[1,2048,768]{2,1,0:T(8,128)(2,1)}, u32[]{:S(2)}) copy-start(bf16[1,2048,768]{2,1,0:T(8,128)(2,1)} %param.14) | copy-start | bytes 9437188
  174.2 4.7 %copy-start.13 = (f32[1152,768]{0,1:T(8,128)}, f32[1152,768]{0,1:T(8,128)S(1)}, u32[]{:S(2)}) copy-start(f32[1152,768]{0,1:T(8,128)S(1)} %convolution_bitcast_fusion) | copy-start | bytes 10616836
  174.2 4.7 %copy-start.6 = (bf16[96,8,16,128]{3,2,1,0:T(8,128)(2,1)S(1)}, bf16[96,8,16,128]{3,2,1,0:T(8,128)(2,1)}, u32[]{:S(2)}) copy-start(bf16[96,8,16,128]{3,2,1,0:T(8,128)(2,1)} %copy.116) | copy-start | bytes 9437188
  178.9 7.9 %copy-start.14 = (f32[1152,768]{0,1:T(8,128)}, f32[1152,768]{0,1:T(8,128)S(1)}, u32[]{:S(2)}) copy-start(f32[1152,768]{0,1:T(8,128)S(1)} %convolution_bitcast_fusion.1) | copy-start | bytes 10616836
  187.7 43.6 %all-to-all-start.3 = ((bf16[128,1,9]{2,1,0:T(2,128)(2,1)}), bf16[128,1,9]{2,1,0:T(2,128)(2,1)S(1)}, u32[]{:S(2)}, u32[]{:S(2)}) async-start(bf16[128,1,9]{2,1,0:T(2,128)(2,1)} %convert_element_type.120), calls=%async_computation.3 | async-start | bytes 131072 | tf_op jit(solution)/shard_map/all_to_all | solution.py:110
  207.0 5.6 %copy-start.11 = (bf16[1,2048,768]{2,1,0:T(8,128)(2,1)S(1)}, bf16[1,2048,768]{2,1,0:T(8,128)(2,1)}, u32[]{:S(2)}) copy-start(bf16[1,2048,768]{2,1,0:T(8,128)(2,1)} %param.14) | copy-start | bytes 9437188
  207.0 5.6 %copy-start.15 = (bf16[1152,768,1]{0,1,2:T(8,128)(2,1)S(1)}, bf16[1152,768,1]{0,1,2:T(8,128)(2,1)}, u32[]{:S(2)}) copy-start(bf16[1152,768,1]{0,1,2:T(8,128)(2,1)} %get-tuple-element.36) | copy-start | bytes 5308420
  231.3 67.6 %all-to-all-start.2 = ((bf16[128,9,16,128]{3,2,1,0:T(8,128)(2,1)}), bf16[128,9,16,128]{3,2,1,0:T(8,128)(2,1)}, u32[]{:S(2)}, u32[]{:S(2)}) async-start(bf16[128,9,16,128]{3,2,1,0:T(8,128)(2,1)} %bitcast.70), calls=%async_computation.2 | async-start | bytes 9437184 | tf_op jit(solution)/shard_map/all_to_all | solution.py:107
  248.0 6.9 %copy-start.12 = (bf16[1152,768]{0,1:T(8,128)(2,1)S(1)}, bf16[1152,768]{0,1:T(8,128)(2,1)}, u32[]{:S(2)}) copy-start(bf16[1152,768]{0,1:T(8,128)(2,1)} %get-tuple-element.33) | copy-start | bytes 5308420
  264.8 7.6 %copy-start.3 = (bf16[128,2048]{1,0:T(8,128)(2,1)S(1)}, bf16[128,2048]{1,0:T(8,128)(2,1)}, u32[]{:S(2)}) copy-start(bf16[128,2048]{1,0:T(8,128)(2,1)} %param.8) | copy-start | bytes 1572868
  309.6 3.5 copy-start.8
  316.2 29.5 %all-to-all-start.4 = ((f32[128,17,128]{2,1,0:T(8,128)}), f32[128,17,128]{2,1,0:T(8,128)S(1)}, u32[]{:S(2)}, u32[]{:S(2)}) async-start(f32[128,17,128]{2,1,0:T(8,128)} %pad_maximum_fusion), calls=%async_computation.4 | async-start | bytes 3145728 | tf_op jit(solution)/shard_map/all_to_all | solution.py:125
  347.2 29.8 %all-to-all-start.5 = ((f32[128,17,128]{2,1,0:T(8,128)}), f32[128,17,128]{2,1,0:T(8,128)}, u32[]{:S(2)}, u32[]{:S(2)}) async-start(f32[128,17,128]{2,1,0:T(8,128)} %broadcast_in_dim.39), calls=%async_computation.5 | async-start | bytes 3145728 | tf_op jit(solution)/shard_map/all_to_all | solution.py:126
  353.1 9.5 %copy-start.4 = (f32[768,2048]{0,1:S(1)}, f32[768,2048]{0,1}, u32[]{:S(2)}) copy-start(f32[768,2048]{0,1} %fusion.25) | copy-start | bytes 18874372
  364.6 16.6 %copy-start.1 = (bf16[1,2048,768]{2,1,0:T(8,128)(2,1)S(1)}, bf16[1,2048,768]{2,1,0:T(8,128)(2,1)}, u32[]{:S(2)}) copy-start(bf16[1,2048,768]{2,1,0:T(8,128)(2,1)} %param.13) | copy-start | bytes 9437188

commit v4 on v2

--- a/solution.py
+++ b/solution.py
@@ -113,7 +113,9 @@
     gain_per = model_width // n_dev
     gain_rows = jnp.pad(gain_part.reshape(n_dev, 1, gain_per), ((0, 0), (0, 0), (0, experts - gain_per)))
     send_sum = jnp.concatenate([router_part.reshape(n_dev, rows_per, experts), gain_rows], axis=1)
-    part_sum = jnp.sum(lax.all_to_all(send_sum, axes, 0, 0, tiled=True), axis=0)
+    part_sum = jnp.sum(
+        lax.all_to_all(send_sum.astype(bf16), axes, 0, 0, tiled=True).astype(f32), axis=0
+    )
     whole = lax.all_to_all(
         jnp.broadcast_to(part_sum[None], (n_dev,) + part_sum.shape), axes, 0, 0, tiled=True
     )

time: 377 us -> 368 us (0.976)
  waiting for transfers between devices: 115 us -> 108 us
    all_to_all x1, waiting for transfers between devices: 12.6 us -> 7.55 us  [local(): lax.all_to_all(send_sum.astype(bf16), axes, 0, 0, tiled=True).astype(f32)]
  transfers between devices with their start and end apart: 7 -> 7, of which waited for: 5 -> 5; matrix products, arithmetic and copies ran while one was open for 40% -> 41% of each run, Pallas kernels for 0% -> 0%
where the time goes in v4:
time: 368 us; the launch traced here: 362 us
  waiting for transfers between devices  108 us (29%)
  local copies, waits for them, and re-layouts  90.8 us (25%)
  matrix products  78.1 us (21%)
  starting transfers between devices  54.4 us (15%)
  other arithmetic  29.8 us (8%)
    dot_general x12, matrix products, dims(): lax.dot_general(left, right, ((left_dims, right_dims), ((), ())), preferr...  65.1 us
    all_to_all x1, waiting for transfers between devices, local(): recv_x = lax.all_to_all(send_x, axes, 0, 0, tiled=True)  40.5 us
    all_to_all x1, waiting for transfers between devices, local(): recv_y = lax.all_to_all(send_y, axes, 0, 0, tiled=True)  30.2 us
    all_to_all x1, waiting for transfers between devices, local(): lax.all_to_all(grad_inputs.reshape(experts, capacity, chunks, lanes), axe...  23.2 us
    convert_element_type x1, local copies, waits for them, and re-layouts, expert_backward(): grad_inputs = (dims(grad_pre_gate, gate3, (1,), (2,)) + dims(grad_pre_up,...  14.3 us
    convert_element_type x1, local copies, waits for them, and re-layouts, local(): dims(sel_tok, normed3, (1,), (0,)).astype(bf16)  14.1 us
    convert_element_type x1, local copies, waits for them, and re-layouts, local(): dims(sel_tok, grads3, (1,), (0,)).astype(bf16)  14.1 us
    all_to_all x1, starting transfers between devices, local(): lax.all_to_all(send_p.reshape(experts, capacity), axes, 0, 0, tiled=True)  11.8 us
  transfers between devices with their start and end apart: 7, of which 5 were waited for; matrix products, arithmetic and copies ran while one was open for 41% of the time, Pallas kernels for 0%

profile of v4, /device:TPU:1, one launch (start us, length us, event | category | flops | bytes accessed | tf_op | source)
XLA Modules:
  0.0 362.2 jit_solution(5266477243423179028)
XLA Ops:
  8.1 8.7 %select_reduce_fusion = bf16[1152]{0:T(1024)(128)(2,1)S(1)} fusion(f32[128,8]{0,1:T(8,128)S(1)} %convert_convert_fusion, s32[128,8]{0,1:T(8,128)S(1)} %get-tuple-element.39), kind=kLoop, calls=%fused_computation.7 | loop fusion | flops 3537792 | bytes 10496 | tf_op jit(solution)/shard_map/reduce_sum | solution.py:79
  17.6 11.8 %all-to-all-start = ((bf16[128,1,9]{2,1,0:T(2,128)(2,1)}), bf16[128,1,9]{2,1,0:T(2,128)(2,1)S(1)}, u32[]{:S(2)}, u32[]{:S(2)}) async-start(bf16[128,1,9]{2,1,0:T(2,128)(2,1)} %convert_element_type.152), calls=%async_computation | async-start | bytes 131072 | tf_op jit(solution)/shard_map/all_to_all | solution.py:87
  29.4 4.2 %fusion.2 = pred[1152,128]{1,0:T(8,128)(4,1)S(1)} fusion(s32[128,8]{0,1:T(8,128)S(1)} %get-tuple-element.39), kind=kLoop, calls=%fused_computation.9 | loop fusion | flops 2211840 | bytes 151552 | tf_op jit(solution)/shard_map/reduce_or | solution.py:78
  36.1 14.1 %copy.137 = bf16[1152,16,128]{2,1,0:T(8,128)(2,1)} copy(bf16[1152,16,128]{2,0,1:T(8,128)(2,1)S(1)} %convolution_convert_fusion) | data formatting | bytes 9437184 | tf_op jit(solution)/shard_map/convert_element_type | solution.py:83
  50.2 10.6 %all-to-all-start.2 = ((bf16[128,9,16,128]{3,2,1,0:T(8,128)(2,1)}), bf16[128,9,16,128]{3,2,1,0:T(8,128)(2,1)}, u32[]{:S(2)}, u32[]{:S(2)}) async-start(bf16[128,9,16,128]{3,2,1,0:T(8,128)(2,1)} %bitcast.86), calls=%async_computation.2 | async-start | bytes 9437184 | tf_op jit(solution)/shard_map/all_to_all | solution.py:85
  63.2 14.1 %copy.133 = bf16[1152,16,128]{2,1,0:T(8,128)(2,1)} copy(bf16[1152,16,128]{2,0,1:T(8,128)(2,1)S(1)} %convolution_convert_fusion.1) | data formatting | bytes 9437184 | tf_op jit(solution)/shard_map/convert_element_type | solution.py:84
  77.3 40.5 %all-to-all-done.2 = bf16[128,9,16,128]{3,2,1,0:T(8,128)(2,1)} async-done(((bf16[128,9,16,128]{3,2,1,0:T(8,128)(2,1)}), bf16[128,9,16,128]{3,2,1,0:T(8,128)(2,1)}, u32[]{:S(2)}, u32[]{:S(2)}) %all-to-all-start.2) | async-done | bytes 4718624 | tf_op jit(solution)/shard_map/all_to_all | solution.py:85
  117.8 5.5 %all-to-all-start.1 = ((bf16[128,9,16,128]{3,2,1,0:T(8,128)(2,1)}), bf16[128,9,16,128]{3,2,1,0:T(8,128)(2,1)}, u32[]{:S(2)}, u32[]{:S(2)}) async-start(bf16[128,9,16,128]{3,2,1,0:T(8,128)(2,1)} %bitcast.85), calls=%async_computation.1 | async-start | bytes 9437184 | tf_op jit(solution)/shard_map/all_to_all | solution.py:86
  123.3 4.6 %copy.173 = bf16[96,8,16,128]{3,2,1,0:T(8,128)(2,1)} copy(bf16[96,8,16,128]{3,1,2,0:T(8,128)(2,1)} %bitcast.91) | data formatting | bytes 6291456
  128.3 7.5 %copy.152 = bf16[1152,16,128]{0,2,1:T(8,128)(2,1)} copy(bf16[1152,16,128]{2,1,0:T(8,128)(2,1)} %bitcast.8) | data formatting | bytes 9437184 | tf_op jit(solution)/shard_map/reshape | solution.py:90
  135.8 8.5 %convolution_bitcast_fusion = f32[1152,768]{0,1:T(8,128)} fusion(bf16[1152,16,128]{0,2,1:T(8,128)(2,1)} %copy.152, bf16[16,128,768]{2,1,0:T(8,128)(2,1)S(1)} %bitcast.82), kind=kOutput, calls=%fused_computation.11 | convolution fusion | flops 3623878656 | bytes 11403264 | tf_op jit(solution)/shard_map/dot_general | solution.py:13
  144.3 6.0 %convolution_bitcast_fusion.1 = f32[1152,768]{0,1:T(8,128)} fusion(bf16[1152,16,128]{0,2,1:T(8,128)(2,1)S(1)} %copy-done.4, bf16[16,128,768]{2,1,0:T(8,128)(2,1)S(1)} %bitcast.95), kind=kOutput, calls=%fused_computation.12 | convolution fusion | flops 3623878656 | bytes 11403264 | tf_op jit(solution)/shard_map/dot_general | solution.py:13
  150.3 30.2 %all-to-all-done.1 = bf16[128,9,16,128]{3,2,1,0:T(8,128)(2,1)} async-done(((bf16[128,9,16,128]{3,2,1,0:T(8,128)(2,1)}), bf16[128,9,16,128]{3,2,1,0:T(8,128)(2,1)}, u32[]{:S(2)}, u32[]{:S(2)}) %all-to-all-start.1) | async-done | bytes 4718624 | tf_op jit(solution)/shard_map/all_to_all | solution.py:86
  180.5 12.9 %multiply_reduce_fusion = (bf16[1152]{0:T(1024)(128)(2,1)S(1)}, bf16[1152,768]{0,1:T(8,128)(2,1)}, bf16[1152,768,1]{0,1,2:T(8,128)(2,1)}) fusion(f32[1152,768]{0,1:T(8,128)} %convolution_bitcast_fusion.1, f32[1152,768]{0,1:T(8,128)} %convolution_bitcast_fusion, f32[1152]{0:T(1024)S(1)} %reshape.242, bf16[768,16,128]{2,1,0:T(8,128)(2,1)} %bitcast.92, ...), kind=kOutput, calls=%fused_computation.13 | convolution fusion | flops 3638918144 | bytes 18488064 | tf_op jit(solution)/shard_map/dot_general | solution.py:13
  194.3 5.1 %all-to-all-start.4 = ((bf16[128,1,9]{2,1,0:T(2,128)(2,1)}), bf16[128,1,9]{2,1,0:T(2,128)(2,1)S(1)}, u32[]{:S(2)}, u32[]{:S(2)}) async-start(bf16[128,1,9]{2,1,0:T(2,128)(2,1)} %convert_element_type.153), calls=%async_computation.4 | async-start | bytes 131072 | tf_op jit(solution)/shard_map/all_to_all | solution.py:100
  199.5 5.5 %fusion.10 = f32[1152,16,128]{2,0,1:T(8,128)S(1)} fusion(bf16[16,128,768]{2,1,0:T(8,128)(2,1)S(1)} %bitcast.83, bf16[1152,768]{0,1:T(8,128)(2,1)} %get-tuple-element.41), kind=kOutput, calls=%fused_computation.30 | convolution fusion | flops 3623878656 | bytes 14352384 | tf_op jit(solution)/shard_map/dot_general | solution.py:13
  205.0 4.2 %add_convert_fusion = bf16[1152,16,128]{2,0,1:T(8,128)(2,1)S(1)} fusion(f32[1152,16,128]{2,0,1:T(8,128)S(1)} %fusion.10, bf16[1152,768,1]{0,1,2:T(8,128)(2,1)S(1)} %copy-done.11, bf16[16,128,768]{2,1,0:T(8,128)(2,1)S(1)} %bitcast.96), kind=kOutput, calls=%fused_computation.2 | convolution fusion | flops 3628597248 | bytes 19070976 | tf_op jit(solution)/shard_map/dot_general | solution.py:13
  209.2 14.3 %copy.144 = bf16[1152,16,128]{2,1,0:T(8,128)(2,1)} copy(bf16[1152,16,128]{2,0,1:T(8,128)(2,1)S(1)} %add_convert_fusion) | data formatting | bytes 9437184 | tf_op jit(solution)/shard_map/convert_element_type | solution.py:40
  223.6 10.6 %all-to-all-start.3 = ((bf16[128,9,16,128]{3,2,1,0:T(8,128)(2,1)}), bf16[128,9,16,128]{3,2,1,0:T(8,128)(2,1)}, u32[]{:S(2)}, u32[]{:S(2)}) async-start(bf16[128,9,16,128]{3,2,1,0:T(8,128)(2,1)} %bitcast.84), calls=%async_computation.3 | async-start | bytes 9437184 | tf_op jit(solution)/shard_map/all_to_all | solution.py:97
  234.4 6.7 %multiply_convert_fusion = bf16[1152,16,128]{2,1,0:T(8,128)(2,1)} fusion(f32[1152]{0:T(1024)S(1)} %reshape.242, bf16[128,9,16,128]{3,2,1,0:T(8,128)(2,1)} %all-to-all-done.1), kind=kLoop, calls=%fused_computation.1 | loop fusion | flops 7077888 | bytes 9441792 | tf_op jit(solution)/shard_map/convert_element_type | solution.py:34
  241.1 7.0 %copy.157 = bf16[1152,16,128]{0,2,1:T(8,128)(2,1)} copy(bf16[1152,16,128]{2,1,0:T(8,128)(2,1)} %multiply_convert_fusion) | data formatting | bytes 9437184 | tf_op jit(solution)/shard_map/convert_element_type | solution.py:34
  248.1 11.5 %fusion.12 = f32[768,2048]{0,1} fusion(bf16[1152,2048]{0,1:T(8,128)(2,1)} %bitcast.90, f32[1152,768]{0,1:T(8,128)} %convolution_bitcast_fusion.1, f32[1152,768]{0,1:T(8,128)} %convolution_bitcast_fusion), kind=kOutput, calls=%fused_computation.32 | convolution fusion | flops 3629187072 | bytes 18087936
  260.0 6.8 %gather_fusion = bf16[1024]{0:T(1024)(128)(2,1)S(1)} fusion(bf16[1152]{0:T(1024)(128)(2,1)S(1)} %reshape.238, s32[1024]{0:T(1024)S(1)} %broadcast_clamp_fusion), kind=kCustom, calls=%fused_computation | custom fusion | bytes 8192 | tf_op jit(solution)/shard_map/gather | solution.py:105
  267.9 23.2 %all-to-all-done.3 = bf16[128,9,16,128]{3,2,1,0:T(8,128)(2,1)} async-done(((bf16[128,9,16,128]{3,2,1,0:T(8,128)(2,1)}), bf16[128,9,16,128]{3,2,1,0:T(8,128)(2,1)}, u32[]{:S(2)}, u32[]{:S(2)}) %all-to-all-start.3) | async-done | bytes 4718624 | tf_op jit(solution)/shard_map/all_to_all | solution.py:97
  291.2 7.1 %copy.145 = bf16[16,128,1152]{2,1,0:T(8,128)(2,1)} copy(bf16[16,128,1152]{1,0,2:T(8,128)(2,1)} %bitcast.17) | data formatting | bytes 9437184 | tf_op jit(solution)/shard_map/dot_general | solution.py:13
  304.9 5.5 %all-to-all-start.5 = ((bf16[128,17,128]{2,1,0:T(8,128)(2,1)}), bf16[128,17,128]{2,1,0:T(8,128)(2,1)S(1)}, u32[]{:S(2)}, u32[]{:S(2)}) async-start(bf16[128,17,128]{2,1,0:T(8,128)(2,1)} %fusion.25), calls=%async_computation.5 | async-start | bytes 1572864 | tf_op jit(solution)/shard_map/all_to_all | solution.py:117
  310.5 8.9 %convolution_convert_fusion.4 = bf16[16,128,768]{2,1,0:T(8,128)(2,1)} fusion(bf16[1152,16,128]{0,2,1:T(8,128)(2,1)} %copy.152, bf16[1152,768]{0,1:T(8,128)(2,1)} %get-tuple-element.41), kind=kOutput, calls=%fused_computation.22 | convolution fusion | flops 3625451520 | bytes 9633792 | tf_op jit(solution)/shard_map/dot_general | solution.py:13
  319.3 7.6 %all-to-all-done.5 = bf16[128,17,128]{2,1,0:T(8,128)(2,1)S(1)} async-done(((bf16[128,17,128]{2,1,0:T(8,128)(2,1)}), bf16[128,17,128]{2,1,0:T(8,128)(2,1)S(1)}, u32[]{:S(2)}, u32[]{:S(2)}) %all-to-all-start.5) | async-done | bytes 557088 | tf_op jit(solution)/shard_map/all_to_all | solution.py:117
  328.4 5.3 %all-to-all-start.6 = ((f32[128,17,128]{2,1,0:T(8,128)}), f32[128,17,128]{2,1,0:T(8,128)}, u32[]{:S(2)}, u32[]{:S(2)}) async-start(f32[128,17,128]{2,1,0:T(8,128)} %broadcast_in_dim.64), calls=%async_computation.6 | async-start | bytes 3145728 | tf_op jit(solution)/shard_map/all_to_all | solution.py:119
  333.6 8.2 %convolution_convert_fusion.3 = bf16[16,128,768]{2,1,0:T(8,128)(2,1)} fusion(bf16[1152,16,128]{0,2,1:T(8,128)(2,1)} %copy.152, bf16[1152,768,1]{0,1,2:T(8,128)(2,1)S(1)} %copy-done.12), kind=kOutput, calls=%fused_computation.21 | convolution fusion | flops 3625451520 | bytes 9633792 | tf_op jit(solution)/shard_map/dot_general | solution.py:13
  343.9 4.8 %copy.158 = bf16[1,768,2048]{2,1,0:T(8,128)(2,1)} copy(bf16[1,768,2048]{1,2,0:T(8,128)(2,1)} %bitcast.88) | data formatting | bytes 6291456
  351.4 6.1 %all-to-all-done.6 = f32[128,17,128]{2,1,0:T(8,128)} async-done(((f32[128,17,128]{2,1,0:T(8,128)}), f32[128,17,128]{2,1,0:T(8,128)}, u32[]{:S(2)}, u32[]{:S(2)}) %all-to-all-start.6) | async-done | bytes 1114144 | tf_op jit(solution)/shard_map/all_to_all | solution.py:119
  (81 shorter events, 33.2 us)
Async XLA Ops:
  0.6 135.1 %copy-start = (bf16[1,2048,768]{2,1,0:T(8,128)(2,1)S(1)}, bf16[1,2048,768]{2,1,0:T(8,128)(2,1)}, u32[]{:S(2)}) copy-start(bf16[1,2048,768]{2,1,0:T(8,128)(2,1)} %param.13) | copy-start | bytes 9437188
  0.6 7.4 %copy-start.8 = (s32[128,8]{0,1:T(8,128)S(1)}, s32[128,8]{0,1:T(8,128)}, u32[]{:S(2)}) copy-start(s32[128,8]{0,1:T(8,128)} %param.12) | copy-start | bytes 12292
  0.7 32.9 %copy-start.7 = (f32[2048]{0:T(1024)S(1)}, f32[2048]{0:T(1024)}, u32[]{:S(2)}) copy-start(f32[2048]{0:T(1024)} %param.9) | copy-start | bytes 24580
  5.5 0.8 copy-start.5
  17.6 32.6 %all-to-all-start = ((bf16[128,1,9]{2,1,0:T(2,128)(2,1)}), bf16[128,1,9]{2,1,0:T(2,128)(2,1)S(1)}, u32[]{:S(2)}, u32[]{:S(2)}) async-start(bf16[128,1,9]{2,1,0:T(2,128)(2,1)} %convert_element_type.152), calls=%async_computation | async-start | bytes 131072 | tf_op jit(solution)/shard_map/all_to_all | solution.py:87
  50.2 67.6 %all-to-all-start.2 = ((bf16[128,9,16,128]{3,2,1,0:T(8,128)(2,1)}), bf16[128,9,16,128]{3,2,1,0:T(8,128)(2,1)}, u32[]{:S(2)}, u32[]{:S(2)}) async-start(bf16[128,9,16,128]{3,2,1,0:T(8,128)(2,1)} %bitcast.86), calls=%async_computation.2 | async-start | bytes 9437184 | tf_op jit(solution)/shard_map/all_to_all | solution.py:85
  117.8 62.7 %all-to-all-start.1 = ((bf16[128,9,16,128]{3,2,1,0:T(8,128)(2,1)}), bf16[128,9,16,128]{3,2,1,0:T(8,128)(2,1)}, u32[]{:S(2)}, u32[]{:S(2)}) async-start(bf16[128,9,16,128]{3,2,1,0:T(8,128)(2,1)} %bitcast.85), calls=%async_computation.1 | async-start | bytes 9437184 | tf_op jit(solution)/shard_map/all_to_all | solution.py:86
  135.8 8.5 %copy-start.4 = (bf16[1152,16,128]{0,2,1:T(8,128)(2,1)S(1)}, bf16[1152,16,128]{0,2,1:T(8,128)(2,1)}, u32[]{:S(2)}) copy-start(bf16[1152,16,128]{0,2,1:T(8,128)(2,1)} %copy.152) | copy-start | bytes 14155780
  135.8 8.5 %copy-start.9 = (bf16[1,2048,768]{2,1,0:T(8,128)(2,1)S(1)}, bf16[1,2048,768]{2,1,0:T(8,128)(2,1)}, u32[]{:S(2)}) copy-start(bf16[1,2048,768]{2,1,0:T(8,128)(2,1)} %param.14) | copy-start | bytes 9437188
  194.3 29.3 %all-to-all-start.4 = ((bf16[128,1,9]{2,1,0:T(2,128)(2,1)}), bf16[128,1,9]{2,1,0:T(2,128)(2,1)S(1)}, u32[]{:S(2)}, u32[]{:S(2)}) async-start(bf16[128,1,9]{2,1,0:T(2,128)(2,1)} %convert_element_type.153), calls=%async_computation.4 | async-start | bytes 131072 | tf_op jit(solution)/shard_map/all_to_all | solution.py:100
  199.4 5.6 %copy-start.10 = (bf16[1,2048,768]{2,1,0:T(8,128)(2,1)S(1)}, bf16[1,2048,768]{2,1,0:T(8,128)(2,1)}, u32[]{:S(2)}) copy-start(bf16[1,2048,768]{2,1,0:T(8,128)(2,1)} %param.14) | copy-start | bytes 9437188
  199.5 5.6 %copy-start.11 = (bf16[1152,768,1]{0,1,2:T(8,128)(2,1)S(1)}, bf16[1152,768,1]{0,1,2:T(8,128)(2,1)}, u32[]{:S(2)}) copy-start(bf16[1152,768,1]{0,1,2:T(8,128)(2,1)} %get-tuple-element.42) | copy-start | bytes 5308420
  223.6 67.6 %all-to-all-start.3 = ((bf16[128,9,16,128]{3,2,1,0:T(8,128)(2,1)}), bf16[128,9,16,128]{3,2,1,0:T(8,128)(2,1)}, u32[]{:S(2)}, u32[]{:S(2)}) async-start(bf16[128,9,16,128]{3,2,1,0:T(8,128)(2,1)} %bitcast.84), calls=%async_computation.3 | async-start | bytes 9437184 | tf_op jit(solution)/shard_map/all_to_all | solution.py:97
  260.0 7.5 %copy-start.2 = (bf16[128,2048]{1,0:T(8,128)(2,1)S(1)}, bf16[128,2048]{1,0:T(8,128)(2,1)}, u32[]{:S(2)}) copy-start(bf16[128,2048]{1,0:T(8,128)(2,1)} %param.8) | copy-start | bytes 1572868
  298.3 4.0 %copy-start.6 = (bf16[2048,128]{1,0:T(8,128)(2,1)S(1)}, bf16[2048,128]{1,0:T(8,128)(2,1)}, u32[]{:S(2)}) copy-start(bf16[2048,128]{1,0:T(8,128)(2,1)} %param.10) | copy-start | bytes 1572868
  304.9 22.0 %all-to-all-start.5 = ((bf16[128,17,128]{2,1,0:T(8,128)(2,1)}), bf16[128,17,128]{2,1,0:T(8,128)(2,1)S(1)}, u32[]{:S(2)}, u32[]{:S(2)}) async-start(bf16[128,17,128]{2,1,0:T(8,128)(2,1)} %fusion.25), calls=%async_computation.5 | async-start | bytes 1572864 | tf_op jit(solution)/shard_map/all_to_all | solution.py:117
  319.3 14.3 %copy-start.12 = (bf16[1152,768,1]{0,1,2:T(8,128)(2,1)S(1)}, bf16[1152,768,1]{0,1,2:T(8,128)(2,1)}, u32[]{:S(2)}) copy-start(bf16[1152,768,1]{0,1,2:T(8,128)(2,1)} %get-tuple-element.42) | copy-start | bytes 5308420
  328.4 29.2 %all-to-all-start.6 = ((f32[128,17,128]{2,1,0:T(8,128)}), f32[128,17,128]{2,1,0:T(8,128)}, u32[]{:S(2)}, u32[]{:S(2)}) async-start(f32[128,17,128]{2,1,0:T(8,128)} %broadcast_in_dim.64), calls=%async_computation.6 | async-start | bytes 3145728 | tf_op jit(solution)/shard_map/all_to_all | solution.py:119
  333.6 8.2 %copy-start.3 = (f32[768,2048]{0,1:S(1)}, f32[768,2048]{0,1}, u32[]{:S(2)}) copy-start(f32[768,2048]{0,1} %fusion.12) | copy-start | bytes 18874372
  343.9 17.8 %copy-start.1 = (bf16[1,2048,768]{2,1,0:T(8,128)(2,1)S(1)}, bf16[1,2048,768]{2,1,0:T(8,128)(2,1)}, u32[]{:S(2)}) copy-start(bf16[1,2048,768]{2,1,0:T(8,128)(2,1)} %param.13) | copy-start | bytes 9437188

commit v5 on v4

--- a/solution.py
+++ b/solution.py
@@ -117,8 +117,12 @@
         lax.all_to_all(send_sum.astype(bf16), axes, 0, 0, tiled=True).astype(f32), axis=0
     )
     whole = lax.all_to_all(
-        jnp.broadcast_to(part_sum[None], (n_dev,) + part_sum.shape), axes, 0, 0, tiled=True
-    )
+        jnp.broadcast_to(part_sum.astype(bf16)[None], (n_dev,) + part_sum.shape),
+        axes,
+        0,
+        0,
+        tiled=True,
+    ).astype(f32)
     grad_router = whole[:, :rows_per, :].reshape(model_width, experts)
     grad_gain = whole[:, rows_per, :gain_per].reshape(model_width)
     scaled = norm_gain * grad_normed

time: 368 us -> 360 us (0.978)
  waiting for transfers between devices: 108 us -> 104 us
    all_to_all x1, waiting for transfers between devices: 23.2 us -> 13 us  [local(): lax.all_to_all(grad_inputs.reshape(experts, capacity, chunks, lanes), axe...]
    all_to_all x1, waiting for transfers between devices: 6.1 us -> 13.5 us  [local(): lax.all_to_all(jnp.broadcast_to(part_sum.astype(bf16)[None], (n_dev,) + p...]
    unnamed x29 -> x25, local copies, waits for them, and re-layouts: 11.2 us -> 9.23 us
where the time goes in v5:
time: 360 us; the launch traced here: 354 us
  waiting for transfers between devices  104 us (29%)
  local copies, waits for them, and re-layouts  87.2 us (24%)
  matrix products  77.4 us (22%)
  starting transfers between devices  54.4 us (15%)
  other arithmetic  29.6 us (8%)
    dot_general x12, matrix products, dims(): lax.dot_general(left, right, ((left_dims, right_dims), ((), ())), preferr...  66.2 us
    all_to_all x1, waiting for transfers between devices, local(): recv_x = lax.all_to_all(send_x, axes, 0, 0, tiled=True)  40.3 us
    all_to_all x1, waiting for transfers between devices, local(): recv_y = lax.all_to_all(send_y, axes, 0, 0, tiled=True)  30.2 us
    convert_element_type x1, local copies, waits for them, and re-layouts, local(): dims(sel_tok, grads3, (1,), (0,)).astype(bf16)  14.2 us
    convert_element_type x1, local copies, waits for them, and re-layouts, expert_backward(): grad_inputs = (dims(grad_pre_gate, gate3, (1,), (2,)) + dims(grad_pre_up,...  14.2 us
    convert_element_type x1, local copies, waits for them, and re-layouts, local(): dims(sel_tok, normed3, (1,), (0,)).astype(bf16)  14.1 us
    all_to_all x1, waiting for transfers between devices, local(): lax.all_to_all(jnp.broadcast_to(part_sum.astype(bf16)[None], (n_dev,) + p...  13.5 us
    all_to_all x1, waiting for transfers between devices, local(): lax.all_to_all(grad_inputs.reshape(experts, capacity, chunks, lanes), axe...  13 us
  transfers between devices with their start and end apart: 7, of which 5 were waited for; matrix products, arithmetic and copies ran while one was open for 41% of the time, Pallas kernels for 0%

profile of v5, /device:TPU:1, one launch (start us, length us, event | category | flops | bytes accessed | tf_op | source)
XLA Modules:
  0.0 354.3 jit_solution(10710633920303547773)
XLA Ops:
  8.1 8.7 %select_reduce_fusion = bf16[1152]{0:T(1024)(128)(2,1)S(1)} fusion(f32[128,8]{0,1:T(8,128)S(1)} %convert_convert_fusion, s32[128,8]{0,1:T(8,128)S(1)} %get-tuple-element.39), kind=kLoop, calls=%fused_computation.7 | loop fusion | flops 3537792 | bytes 10496 | tf_op jit(solution)/shard_map/reduce_sum | solution.py:79
  17.6 11.8 %all-to-all-start = ((bf16[128,1,9]{2,1,0:T(2,128)(2,1)}), bf16[128,1,9]{2,1,0:T(2,128)(2,1)S(1)}, u32[]{:S(2)}, u32[]{:S(2)}) async-start(bf16[128,1,9]{2,1,0:T(2,128)(2,1)} %convert_element_type.154), calls=%async_computation | async-start | bytes 131072 | tf_op jit(solution)/shard_map/all_to_all | solution.py:87
  29.4 4.2 %fusion.2 = pred[1152,128]{1,0:T(8,128)(4,1)S(1)} fusion(s32[128,8]{0,1:T(8,128)S(1)} %get-tuple-element.39), kind=kLoop, calls=%fused_computation.9 | loop fusion | flops 2211840 | bytes 151552 | tf_op jit(solution)/shard_map/reduce_or | solution.py:78
  36.1 14.1 %copy.137 = bf16[1152,16,128]{2,1,0:T(8,128)(2,1)} copy(bf16[1152,16,128]{2,0,1:T(8,128)(2,1)S(1)} %convolution_convert_fusion) | data formatting | bytes 9437184 | tf_op jit(solution)/shard_map/convert_element_type | solution.py:83
  50.3 10.7 %all-to-all-start.2 = ((bf16[128,9,16,128]{3,2,1,0:T(8,128)(2,1)}), bf16[128,9,16,128]{3,2,1,0:T(8,128)(2,1)}, u32[]{:S(2)}, u32[]{:S(2)}) async-start(bf16[128,9,16,128]{3,2,1,0:T(8,128)(2,1)} %bitcast.86), calls=%async_computation.2 | async-start | bytes 9437184 | tf_op jit(solution)/shard_map/all_to_all | solution.py:85
  63.4 14.2 %copy.133 = bf16[1152,16,128]{2,1,0:T(8,128)(2,1)} copy(bf16[1152,16,128]{2,0,1:T(8,128)(2,1)S(1)} %convolution_convert_fusion.1) | data formatting | bytes 9437184 | tf_op jit(solution)/shard_map/convert_element_type | solution.py:84
  77.7 40.3 %all-to-all-done.2 = bf16[128,9,16,128]{3,2,1,0:T(8,128)(2,1)} async-done(((bf16[128,9,16,128]{3,2,1,0:T(8,128)(2,1)}), bf16[128,9,16,128]{3,2,1,0:T(8,128)(2,1)}, u32[]{:S(2)}, u32[]{:S(2)}) %all-to-all-start.2) | async-done | bytes 4718624 | tf_op jit(solution)/shard_map/all_to_all | solution.py:85
  118.0 5.5 %all-to-all-start.1 = ((bf16[128,9,16,128]{3,2,1,0:T(8,128)(2,1)}), bf16[128,9,16,128]{3,2,1,0:T(8,128)(2,1)}, u32[]{:S(2)}, u32[]{:S(2)}) async-start(bf16[128,9,16,128]{3,2,1,0:T(8,128)(2,1)} %bitcast.85), calls=%async_computation.1 | async-start | bytes 9437184 | tf_op jit(solution)/shard_map/all_to_all | solution.py:86
  123.5 4.6 %copy.173 = bf16[96,8,16,128]{3,2,1,0:T(8,128)(2,1)} copy(bf16[96,8,16,128]{3,1,2,0:T(8,128)(2,1)} %bitcast.91) | data formatting | bytes 6291456
  128.5 7.2 %copy.152 = bf16[1152,16,128]{0,2,1:T(8,128)(2,1)} copy(bf16[1152,16,128]{2,1,0:T(8,128)(2,1)} %bitcast.8) | data formatting | bytes 9437184 | tf_op jit(solution)/shard_map/reshape | solution.py:90
  135.8 8.7 %convolution_bitcast_fusion = f32[1152,768]{0,1:T(8,128)} fusion(bf16[1152,16,128]{0,2,1:T(8,128)(2,1)} %copy.152, bf16[16,128,768]{2,1,0:T(8,128)(2,1)S(1)} %bitcast.82), kind=kOutput, calls=%fused_computation.11 | convolution fusion | flops 3623878656 | bytes 11403264 | tf_op jit(solution)/shard_map/dot_general | solution.py:13
  144.5 6.1 %convolution_bitcast_fusion.1 = f32[1152,768]{0,1:T(8,128)} fusion(bf16[1152,16,128]{0,2,1:T(8,128)(2,1)S(1)} %copy-done.3, bf16[16,128,768]{2,1,0:T(8,128)(2,1)S(1)} %bitcast.95), kind=kOutput, calls=%fused_computation.12 | convolution fusion | flops 3623878656 | bytes 11403264 | tf_op jit(solution)/shard_map/dot_general | solution.py:13
  150.6 30.2 %all-to-all-done.1 = bf16[128,9,16,128]{3,2,1,0:T(8,128)(2,1)} async-done(((bf16[128,9,16,128]{3,2,1,0:T(8,128)(2,1)}), bf16[128,9,16,128]{3,2,1,0:T(8,128)(2,1)}, u32[]{:S(2)}, u32[]{:S(2)}) %all-to-all-start.1) | async-done | bytes 4718624 | tf_op jit(solution)/shard_map/all_to_all | solution.py:86
  180.7 13.2 %multiply_reduce_fusion = (bf16[1152]{0:T(1024)(128)(2,1)S(1)}, bf16[1152,768]{0,1:T(8,128)(2,1)}, bf16[1152,768,1]{0,1,2:T(8,128)(2,1)}) fusion(f32[1152,768]{0,1:T(8,128)} %convolution_bitcast_fusion.1, f32[1152,768]{0,1:T(8,128)} %convolution_bitcast_fusion, f32[1152]{0:T(1024)S(1)} %reshape.242, bf16[768,16,128]{2,1,0:T(8,128)(2,1)} %bitcast.92, ...), kind=kOutput, calls=%fused_computation.13 | convolution fusion | flops 3638918144 | bytes 18488064 | tf_op jit(solution)/shard_map/dot_general | solution.py:13
  194.8 5.1 %all-to-all-start.4 = ((bf16[128,1,9]{2,1,0:T(2,128)(2,1)}), bf16[128,1,9]{2,1,0:T(2,128)(2,1)S(1)}, u32[]{:S(2)}, u32[]{:S(2)}) async-start(bf16[128,1,9]{2,1,0:T(2,128)(2,1)} %convert_element_type.155), calls=%async_computation.4 | async-start | bytes 131072 | tf_op jit(solution)/shard_map/all_to_all | solution.py:100
  199.9 5.5 %fusion.10 = f32[1152,16,128]{2,0,1:T(8,128)S(1)} fusion(bf16[16,128,768]{2,1,0:T(8,128)(2,1)S(1)} %bitcast.83, bf16[1152,768]{0,1:T(8,128)(2,1)} %get-tuple-element.41), kind=kOutput, calls=%fused_computation.30 | convolution fusion | flops 3623878656 | bytes 14352384 | tf_op jit(solution)/shard_map/dot_general | solution.py:13
  205.5 4.2 %add_convert_fusion = bf16[1152,16,128]{2,0,1:T(8,128)(2,1)S(1)} fusion(f32[1152,16,128]{2,0,1:T(8,128)S(1)} %fusion.10, bf16[1152,768,1]{0,1,2:T(8,128)(2,1)S(1)} %copy-done.10, bf16[16,128,768]{2,1,0:T(8,128)(2,1)S(1)} %bitcast.96), kind=kOutput, calls=%fused_computation.2 | convolution fusion | flops 3628597248 | bytes 19070976 | tf_op jit(solution)/shard_map/dot_general | solution.py:13
  209.7 14.2 %copy.144 = bf16[1152,16,128]{2,1,0:T(8,128)(2,1)} copy(bf16[1152,16,128]{2,0,1:T(8,128)(2,1)S(1)} %add_convert_fusion) | data formatting | bytes 9437184 | tf_op jit(solution)/shard_map/convert_element_type | solution.py:40
  223.9 10.5 %all-to-all-start.3 = ((bf16[128,9,16,128]{3,2,1,0:T(8,128)(2,1)}), bf16[128,9,16,128]{3,2,1,0:T(8,128)(2,1)}, u32[]{:S(2)}, u32[]{:S(2)}) async-start(bf16[128,9,16,128]{3,2,1,0:T(8,128)(2,1)} %bitcast.84), calls=%async_computation.3 | async-start | bytes 9437184 | tf_op jit(solution)/shard_map/all_to_all | solution.py:97
  234.6 6.7 %multiply_convert_fusion = bf16[1152,16,128]{2,1,0:T(8,128)(2,1)} fusion(f32[1152]{0:T(1024)S(1)} %reshape.242, bf16[128,9,16,128]{3,2,1,0:T(8,128)(2,1)} %all-to-all-done.1), kind=kLoop, calls=%fused_computation.1 | loop fusion | flops 7077888 | bytes 9441792 | tf_op jit(solution)/shard_map/convert_element_type | solution.py:34
  241.3 7.1 %copy.157 = bf16[1152,16,128]{0,2,1:T(8,128)(2,1)} copy(bf16[1152,16,128]{2,1,0:T(8,128)(2,1)} %multiply_convert_fusion) | data formatting | bytes 9437184 | tf_op jit(solution)/shard_map/convert_element_type | solution.py:34
  248.4 9.5 %fusion.12 = f32[768,2048]{0,1:S(1)} fusion(bf16[1152,2048]{0,1:T(8,128)(2,1)} %bitcast.90, f32[1152,768]{0,1:T(8,128)} %convolution_bitcast_fusion.1, f32[1152,768]{0,1:T(8,128)} %convolution_bitcast_fusion), kind=kOutput, calls=%fused_computation.32 | convolution fusion | flops 3629187072 | bytes 18087936
  261.3 8.9 %convolution_convert_fusion.4 = bf16[16,128,768]{2,1,0:T(8,128)(2,1)} fusion(bf16[1152,16,128]{0,2,1:T(8,128)(2,1)} %copy.152, bf16[1152,768]{0,1:T(8,128)(2,1)} %get-tuple-element.41), kind=kOutput, calls=%fused_computation.22 | convolution fusion | flops 3625451520 | bytes 9633792 | tf_op jit(solution)/shard_map/dot_general | solution.py:13
  270.5 6.8 %gather_fusion = bf16[1024]{0:T(1024)(128)(2,1)S(1)} fusion(bf16[1152]{0:T(1024)(128)(2,1)S(1)} %reshape.238, s32[1024]{0:T(1024)S(1)} %broadcast_clamp_fusion), kind=kCustom, calls=%fused_computation | custom fusion | bytes 8192 | tf_op jit(solution)/shard_map/gather | solution.py:105
  278.4 13.0 %all-to-all-done.3 = bf16[128,9,16,128]{3,2,1,0:T(8,128)(2,1)} async-done(((bf16[128,9,16,128]{3,2,1,0:T(8,128)(2,1)}), bf16[128,9,16,128]{3,2,1,0:T(8,128)(2,1)}, u32[]{:S(2)}, u32[]{:S(2)}) %all-to-all-start.3) | async-done | bytes 4718624 | tf_op jit(solution)/shard_map/all_to_all | solution.py:97
  291.4 7.1 %copy.145 = bf16[16,128,1152]{2,1,0:T(8,128)(2,1)} copy(bf16[16,128,1152]{1,0,2:T(8,128)(2,1)} %bitcast.17) | data formatting | bytes 9437184 | tf_op jit(solution)/shard_map/dot_general | solution.py:13
  298.5 4.0 %fusion.35 = f32[128,2048]{1,0:T(8,128)S(1)} fusion(bf16[2048,1152]{1,0:T(8,128)(2,1)} %bitcast.87, pred[1152,128]{1,0:T(8,128)(4,1)S(1)} %fusion.2), kind=kOutput, calls=%fused_computation.62 | convolution fusion | flops 604127232 | bytes 5914624 | tf_op jit(solution)/shard_map/dot_general | solution.py:13
  305.2 5.5 %all-to-all-start.5 = ((bf16[128,17,128]{2,1,0:T(8,128)(2,1)}), bf16[128,17,128]{2,1,0:T(8,128)(2,1)S(1)}, u32[]{:S(2)}, u32[]{:S(2)}) async-start(bf16[128,17,128]{2,1,0:T(8,128)(2,1)} %fusion.25), calls=%async_computation.5 | async-start | bytes 1572864 | tf_op jit(solution)/shard_map/all_to_all | solution.py:117
  310.6 8.9 %convolution_convert_fusion.3 = bf16[16,128,768]{2,1,0:T(8,128)(2,1)} fusion(bf16[1152,16,128]{0,2,1:T(8,128)(2,1)} %copy.152, bf16[1152,768,1]{0,1,2:T(8,128)(2,1)} %get-tuple-element.42), kind=kOutput, calls=%fused_computation.21 | convolution fusion | flops 3625451520 | bytes 9633792 | tf_op jit(solution)/shard_map/dot_general | solution.py:13
  319.5 7.6 %all-to-all-done.5 = bf16[128,17,128]{2,1,0:T(8,128)(2,1)S(1)} async-done(((bf16[128,17,128]{2,1,0:T(8,128)(2,1)}), bf16[128,17,128]{2,1,0:T(8,128)(2,1)S(1)}, u32[]{:S(2)}, u32[]{:S(2)}) %all-to-all-start.5) | async-done | bytes 557088 | tf_op jit(solution)/shard_map/all_to_all | solution.py:117
  328.2 5.2 %all-to-all-start.6 = ((bf16[128,17,128]{2,1,0:T(8,128)(2,1)}), bf16[128,17,128]{2,1,0:T(8,128)(2,1)}, u32[]{:S(2)}, u32[]{:S(2)}) async-start(bf16[128,17,128]{2,1,0:T(8,128)(2,1)} %broadcast_in_dim.64), calls=%async_computation.6 | async-start | bytes 1572864 | tf_op jit(solution)/shard_map/all_to_all | solution.py:119
  336.4 13.5 %all-to-all-done.6 = bf16[128,17,128]{2,1,0:T(8,128)(2,1)} async-done(((bf16[128,17,128]{2,1,0:T(8,128)(2,1)}), bf16[128,17,128]{2,1,0:T(8,128)(2,1)}, u32[]{:S(2)}, u32[]{:S(2)}) %all-to-all-start.6) | async-done | bytes 557088 | tf_op jit(solution)/shard_map/all_to_all | solution.py:119
  (78 shorter events, 30.2 us)
Async XLA Ops:
  0.6 135.1 %copy-start = (bf16[1,2048,768]{2,1,0:T(8,128)(2,1)S(1)}, bf16[1,2048,768]{2,1,0:T(8,128)(2,1)}, u32[]{:S(2)}) copy-start(bf16[1,2048,768]{2,1,0:T(8,128)(2,1)} %param.13) | copy-start | bytes 9437188
  0.6 7.4 %copy-start.7 = (s32[128,8]{0,1:T(8,128)S(1)}, s32[128,8]{0,1:T(8,128)}, u32[]{:S(2)}) copy-start(s32[128,8]{0,1:T(8,128)} %param.12) | copy-start | bytes 12292
  0.7 33.0 %copy-start.6 = (f32[2048]{0:T(1024)S(1)}, f32[2048]{0:T(1024)}, u32[]{:S(2)}) copy-start(f32[2048]{0:T(1024)} %param.9) | copy-start | bytes 24580
  5.5 0.8 copy-start.4
  17.6 32.6 %all-to-all-start = ((bf16[128,1,9]{2,1,0:T(2,128)(2,1)}), bf16[128,1,9]{2,1,0:T(2,128)(2,1)S(1)}, u32[]{:S(2)}, u32[]{:S(2)}) async-start(bf16[128,1,9]{2,1,0:T(2,128)(2,1)} %convert_element_type.154), calls=%async_computation | async-start | bytes 131072 | tf_op jit(solution)/shard_map/all_to_all | solution.py:87
  50.3 67.7 %all-to-all-start.2 = ((bf16[128,9,16,128]{3,2,1,0:T(8,128)(2,1)}), bf16[128,9,16,128]{3,2,1,0:T(8,128)(2,1)}, u32[]{:S(2)}, u32[]{:S(2)}) async-start(bf16[128,9,16,128]{3,2,1,0:T(8,128)(2,1)} %bitcast.86), calls=%async_computation.2 | async-start | bytes 9437184 | tf_op jit(solution)/shard_map/all_to_all | solution.py:85
  118.0 62.7 %all-to-all-start.1 = ((bf16[128,9,16,128]{3,2,1,0:T(8,128)(2,1)}), bf16[128,9,16,128]{3,2,1,0:T(8,128)(2,1)}, u32[]{:S(2)}, u32[]{:S(2)}) async-start(bf16[128,9,16,128]{3,2,1,0:T(8,128)(2,1)} %bitcast.85), calls=%async_computation.1 | async-start | bytes 9437184 | tf_op jit(solution)/shard_map/all_to_all | solution.py:86
  135.8 8.7 %copy-start.3 = (bf16[1152,16,128]{0,2,1:T(8,128)(2,1)S(1)}, bf16[1152,16,128]{0,2,1:T(8,128)(2,1)}, u32[]{:S(2)}) copy-start(bf16[1152,16,128]{0,2,1:T(8,128)(2,1)} %copy.152) | copy-start | bytes 14155780
  135.8 8.7 %copy-start.8 = (bf16[1,2048,768]{2,1,0:T(8,128)(2,1)S(1)}, bf16[1,2048,768]{2,1,0:T(8,128)(2,1)}, u32[]{:S(2)}) copy-start(bf16[1,2048,768]{2,1,0:T(8,128)(2,1)} %param.14) | copy-start | bytes 9437188
  194.8 29.1 %all-to-all-start.4 = ((bf16[128,1,9]{2,1,0:T(2,128)(2,1)}), bf16[128,1,9]{2,1,0:T(2,128)(2,1)S(1)}, u32[]{:S(2)}, u32[]{:S(2)}) async-start(bf16[128,1,9]{2,1,0:T(2,128)(2,1)} %convert_element_type.155), calls=%async_computation.4 | async-start | bytes 131072 | tf_op jit(solution)/shard_map/all_to_all | solution.py:100
  199.9 5.6 %copy-start.9 = (bf16[1,2048,768]{2,1,0:T(8,128)(2,1)S(1)}, bf16[1,2048,768]{2,1,0:T(8,128)(2,1)}, u32[]{:S(2)}) copy-start(bf16[1,2048,768]{2,1,0:T(8,128)(2,1)} %param.14) | copy-start | bytes 9437188
  199.9 5.6 %copy-start.10 = (bf16[1152,768,1]{0,1,2:T(8,128)(2,1)S(1)}, bf16[1152,768,1]{0,1,2:T(8,128)(2,1)}, u32[]{:S(2)}) copy-start(bf16[1152,768,1]{0,1,2:T(8,128)(2,1)} %get-tuple-element.42) | copy-start | bytes 5308420
  223.9 67.5 %all-to-all-start.3 = ((bf16[128,9,16,128]{3,2,1,0:T(8,128)(2,1)}), bf16[128,9,16,128]{3,2,1,0:T(8,128)(2,1)}, u32[]{:S(2)}, u32[]{:S(2)}) async-start(bf16[128,9,16,128]{3,2,1,0:T(8,128)(2,1)} %bitcast.84), calls=%async_computation.3 | async-start | bytes 9437184 | tf_op jit(solution)/shard_map/all_to_all | solution.py:97
  270.5 7.5 %copy-start.2 = (bf16[128,2048]{1,0:T(8,128)(2,1)S(1)}, bf16[128,2048]{1,0:T(8,128)(2,1)}, u32[]{:S(2)}) copy-start(bf16[128,2048]{1,0:T(8,128)(2,1)} %param.8) | copy-start | bytes 1572868
  298.5 4.0 %copy-start.5 = (bf16[2048,128]{1,0:T(8,128)(2,1)S(1)}, bf16[2048,128]{1,0:T(8,128)(2,1)}, u32[]{:S(2)}) copy-start(bf16[2048,128]{1,0:T(8,128)(2,1)} %param.10) | copy-start | bytes 1572868
  305.2 21.9 %all-to-all-start.5 = ((bf16[128,17,128]{2,1,0:T(8,128)(2,1)}), bf16[128,17,128]{2,1,0:T(8,128)(2,1)S(1)}, u32[]{:S(2)}, u32[]{:S(2)}) async-start(bf16[128,17,128]{2,1,0:T(8,128)(2,1)} %fusion.25), calls=%async_computation.5 | async-start | bytes 1572864 | tf_op jit(solution)/shard_map/all_to_all | solution.py:117
  328.2 21.6 %all-to-all-start.6 = ((bf16[128,17,128]{2,1,0:T(8,128)(2,1)}), bf16[128,17,128]{2,1,0:T(8,128)(2,1)}, u32[]{:S(2)}, u32[]{:S(2)}) async-start(bf16[128,17,128]{2,1,0:T(8,128)(2,1)} %broadcast_in_dim.64), calls=%async_computation.6 | async-start | bytes 1572864 | tf_op jit(solution)/shard_map/all_to_all | solution.py:119
  333.5 20.6 %copy-start.1 = (bf16[1,2048,768]{2,1,0:T(8,128)(2,1)S(1)}, bf16[1,2048,768]{2,1,0:T(8,128)(2,1)}, u32[]{:S(2)}) copy-start(bf16[1,2048,768]{2,1,0:T(8,128)(2,1)} %param.13) | copy-start | bytes 9437188

commit v6 on v5

--- a/solution.py
+++ b/solution.py
@@ -36,8 +36,10 @@
     grad_up_mat = dims(rows_x, grad_pre_up, (0,), (0,)).astype(jnp.bfloat16)
     grad_down_mat = dims(hidden_act.astype(jnp.bfloat16), scaled_up, (0,), (0,)).astype(jnp.bfloat16)
     grad_inputs = (
-        dims(grad_pre_gate, gate3, (1,), (2,)) + dims(grad_pre_up, up3, (1,), (2,))
-    ).astype(jnp.bfloat16)
+        (dims(grad_pre_gate, gate_mat, (1,), (1,)) + dims(grad_pre_up, up_mat, (1,), (1,)))
+        .astype(jnp.bfloat16)
+        .reshape(slots, chunks, lanes)
+    )
     return (
         grad_gate_mat.reshape(chunks * lanes, ff),
         grad_up_mat.reshape(chunks * lanes, ff),

time: 360 us -> 343 us (0.953)
  local copies, waits for them, and re-layouts: 87.2 us -> 69.6 us
    convert_element_type x1 -> x0, local copies, waits for them, and re-layouts: 14.2 us -> none  [expert_backward(): grad_inputs = (dims(grad_pre_gate, gate3, (1,), (2,)) + dims(grad_pre_up,...]
    dot_general x1 -> x0, local copies, waits for them, and re-layouts: 7.1 us -> none  [dims(): lax.dot_general(left, right, ((left_dims, right_dims), ((), ())), preferr...]
    unnamed x25 -> x24, local copies, waits for them, and re-layouts: 9.23 us -> 12.9 us
  transfers between devices with their start and end apart: 7 -> 7, of which waited for: 5 -> 5; matrix products, arithmetic and copies ran while one was open for 41% -> 40% of each run, Pallas kernels for 0% -> 0%
where the time goes in v6:
time: 343 us; the launch traced here: 338 us
  waiting for transfers between devices  104 us (30%)
  matrix products  78 us (23%)
  local copies, waits for them, and re-layouts  69.6 us (20%)
  starting transfers between devices  54.8 us (16%)
  other arithmetic  29.6 us (9%)
    dot_general x12, matrix products, dims(): lax.dot_general(left, right, ((left_dims, right_dims), ((), ())), preferr...  66.9 us
    all_to_all x1, waiting for transfers between devices, local(): recv_x = lax.all_to_all(send_x, axes, 0, 0, tiled=True)  40.3 us
    all_to_all x1, waiting for transfers between devices, local(): recv_y = lax.all_to_all(send_y, axes, 0, 0, tiled=True)  30.2 us
    convert_element_type x1, local copies, waits for them, and re-layouts, local(): dims(sel_tok, grads3, (1,), (0,)).astype(bf16)  14.2 us
    convert_element_type x1, local copies, waits for them, and re-layouts, local(): dims(sel_tok, normed3, (1,), (0,)).astype(bf16)  14.1 us
    all_to_all x1, waiting for transfers between devices, local(): lax.all_to_all(jnp.broadcast_to(part_sum.astype(bf16)[None], (n_dev,) + p...  13.5 us
    all_to_all x1, waiting for transfers between devices, local(): lax.all_to_all(grad_inputs.reshape(experts, capacity, chunks, lanes), axe...  12.9 us
    unnamed x24, local copies, waits for them, and re-layouts  12.9 us
  transfers between devices with their start and end apart: 7, of which 5 were waited for; matrix products, arithmetic and copies ran while one was open for 40% of the time, Pallas kernels for 0%

profile of v6, /device:TPU:1, one launch (start us, length us, event | category | flops | bytes accessed | tf_op | source)
XLA Modules:
  0.0 337.7 jit_solution(15312737016077863701)
XLA Ops:
  8.1 8.7 %select_reduce_fusion = bf16[1152]{0:T(1024)(128)(2,1)S(1)} fusion(f32[128,8]{0,1:T(8,128)S(1)} %convert_convert_fusion, s32[128,8]{0,1:T(8,128)S(1)} %get-tuple-element.39), kind=kLoop, calls=%fused_computation.10 | loop fusion | flops 3537792 | bytes 10496 | tf_op jit(solution)/shard_map/reduce_sum | solution.py:81
  17.6 11.9 %all-to-all-start = ((bf16[128,1,9]{2,1,0:T(2,128)(2,1)}), bf16[128,1,9]{2,1,0:T(2,128)(2,1)S(1)}, u32[]{:S(2)}, u32[]{:S(2)}) async-start(bf16[128,1,9]{2,1,0:T(2,128)(2,1)} %convert_element_type.154), calls=%async_computation | async-start | bytes 131072 | tf_op jit(solution)/shard_map/all_to_all | solution.py:89
  29.5 4.2 %fusion.5 = pred[1152,128]{1,0:T(8,128)(4,1)S(1)} fusion(s32[128,8]{0,1:T(8,128)S(1)} %get-tuple-element.39), kind=kLoop, calls=%fused_computation.12 | loop fusion | flops 2211840 | bytes 151552 | tf_op jit(solution)/shard_map/reduce_or | solution.py:80
  36.2 14.1 %copy.123 = bf16[1152,16,128]{2,1,0:T(8,128)(2,1)} copy(bf16[1152,16,128]{2,0,1:T(8,128)(2,1)S(1)} %convolution_convert_fusion) | data formatting | bytes 9437184 | tf_op jit(solution)/shard_map/convert_element_type | solution.py:85
  50.3 10.9 %all-to-all-start.2 = ((bf16[128,9,16,128]{3,2,1,0:T(8,128)(2,1)}), bf16[128,9,16,128]{3,2,1,0:T(8,128)(2,1)}, u32[]{:S(2)}, u32[]{:S(2)}) async-start(bf16[128,9,16,128]{3,2,1,0:T(8,128)(2,1)} %bitcast.94), calls=%async_computation.2 | async-start | bytes 9437184 | tf_op jit(solution)/shard_map/all_to_all | solution.py:87
  63.6 14.2 %copy.119 = bf16[1152,16,128]{2,1,0:T(8,128)(2,1)} copy(bf16[1152,16,128]{2,0,1:T(8,128)(2,1)S(1)} %convolution_convert_fusion.1) | data formatting | bytes 9437184 | tf_op jit(solution)/shard_map/convert_element_type | solution.py:86
  77.9 40.3 %all-to-all-done.2 = bf16[128,9,16,128]{3,2,1,0:T(8,128)(2,1)} async-done(((bf16[128,9,16,128]{3,2,1,0:T(8,128)(2,1)}), bf16[128,9,16,128]{3,2,1,0:T(8,128)(2,1)}, u32[]{:S(2)}, u32[]{:S(2)}) %all-to-all-start.2) | async-done | bytes 4718624 | tf_op jit(solution)/shard_map/all_to_all | solution.py:87
  118.2 5.5 %all-to-all-start.1 = ((bf16[128,9,16,128]{3,2,1,0:T(8,128)(2,1)}), bf16[128,9,16,128]{3,2,1,0:T(8,128)(2,1)}, u32[]{:S(2)}, u32[]{:S(2)}) async-start(bf16[128,9,16,128]{3,2,1,0:T(8,128)(2,1)} %bitcast.93), calls=%async_computation.1 | async-start | bytes 9437184 | tf_op jit(solution)/shard_map/all_to_all | solution.py:88
  123.7 4.6 %copy.151 = bf16[96,8,16,128]{3,2,1,0:T(8,128)(2,1)} copy(bf16[96,8,16,128]{3,1,2,0:T(8,128)(2,1)} %bitcast.98) | data formatting | bytes 6291456
  128.7 7.2 %copy.134 = bf16[1152,16,128]{0,2,1:T(8,128)(2,1)} copy(bf16[1152,16,128]{2,1,0:T(8,128)(2,1)} %bitcast.8) | data formatting | bytes 9437184 | tf_op jit(solution)/shard_map/reshape | solution.py:92
  136.0 8.7 %convolution_bitcast_fusion = f32[1152,768]{0,1:T(8,128)} fusion(bf16[1152,16,128]{0,2,1:T(8,128)(2,1)} %copy.134, bf16[16,128,768]{2,1,0:T(8,128)(2,1)S(1)} %bitcast.91), kind=kOutput, calls=%fused_computation.14 | convolution fusion | flops 3623878656 | bytes 11403264 | tf_op jit(solution)/shard_map/dot_general | solution.py:13
  144.7 6.1 %convolution_bitcast_fusion.1 = f32[1152,768]{0,1:T(8,128)} fusion(bf16[1152,16,128]{0,2,1:T(8,128)(2,1)S(1)} %copy-done.3, bf16[16,128,768]{2,1,0:T(8,128)(2,1)S(1)} %bitcast.102), kind=kOutput, calls=%fused_computation.15 | convolution fusion | flops 3623878656 | bytes 11403264 | tf_op jit(solution)/shard_map/dot_general | solution.py:13
  150.8 30.2 %all-to-all-done.1 = bf16[128,9,16,128]{3,2,1,0:T(8,128)(2,1)} async-done(((bf16[128,9,16,128]{3,2,1,0:T(8,128)(2,1)}), bf16[128,9,16,128]{3,2,1,0:T(8,128)(2,1)}, u32[]{:S(2)}, u32[]{:S(2)}) %all-to-all-start.1) | async-done | bytes 4718624 | tf_op jit(solution)/shard_map/all_to_all | solution.py:88
  180.9 13.0 %multiply_reduce_fusion = (bf16[1152]{0:T(1024)(128)(2,1)S(1)}, bf16[1152,768]{0,1:T(8,128)(2,1)}, bf16[1152,768]{0,1:T(8,128)(2,1)}) fusion(f32[1152,768]{0,1:T(8,128)} %convolution_bitcast_fusion.1, f32[1152,768]{0,1:T(8,128)} %convolution_bitcast_fusion, f32[1152]{0:T(1024)S(1)} %reshape.238, bf16[768,16,128]{2,1,0:T(8,128)(2,1)} %bitcast.99, ...), kind=kOutput, calls=%fused_computation.16 | convolution fusion | flops 3638918144 | bytes 18488064 | tf_op jit(solution)/shard_map/dot_general | solution.py:13
  194.8 5.1 %all-to-all-start.4 = ((bf16[128,1,9]{2,1,0:T(2,128)(2,1)}), bf16[128,1,9]{2,1,0:T(2,128)(2,1)S(1)}, u32[]{:S(2)}, u32[]{:S(2)}) async-start(bf16[128,1,9]{2,1,0:T(2,128)(2,1)} %convert_element_type.155), calls=%async_computation.4 | async-start | bytes 131072 | tf_op jit(solution)/shard_map/all_to_all | solution.py:102
  199.9 5.6 %fusion.11 = f32[1152,2048]{1,0:T(8,128)S(1)} fusion(bf16[1152,768]{0,1:T(8,128)(2,1)} %get-tuple-element.41, bf16[1,2048,768]{2,1,0:T(8,128)(2,1)S(1)} %copy-done), kind=kOutput, calls=%fused_computation.22 | convolution fusion | flops 3623878656 | bytes 14352384 | tf_op jit(solution)/shard_map/dot_general | solution.py:13
  205.5 5.8 %fusion.14 = bf16[144,8,16,128]{3,1,2,0:T(8,128)(2,1)S(1)} fusion(f32[1152,2048]{1,0:T(8,128)S(1)} %fusion.11, bf16[1152,768]{0,1:T(8,128)(2,1)} %get-tuple-element.42, bf16[1,2048,768]{2,1,0:T(8,128)(2,1)S(1)} %copy-done.9), kind=kOutput, calls=%fused_computation.27 | convolution fusion | flops 3628597248 | bytes 19070976 | tf_op jit(solution)/shard_map/dot_general | solution.py:13
  211.3 3.7 %copy.152 = bf16[144,8,16,128]{3,2,1,0:T(8,128)(2,1)} copy(bf16[144,8,16,128]{3,1,2,0:T(8,128)(2,1)S(1)} %fusion.14) | data formatting | bytes 9437184
  215.0 10.7 %all-to-all-start.3 = ((bf16[128,9,16,128]{3,2,1,0:T(8,128)(2,1)}), bf16[128,9,16,128]{3,2,1,0:T(8,128)(2,1)}, u32[]{:S(2)}, u32[]{:S(2)}) async-start(bf16[128,9,16,128]{3,2,1,0:T(8,128)(2,1)} %bitcast.92), calls=%async_computation.3 | async-start | bytes 9437184 | tf_op jit(solution)/shard_map/all_to_all | solution.py:99
  226.0 6.7 %multiply_convert_fusion = bf16[1152,16,128]{2,1,0:T(8,128)(2,1)} fusion(f32[1152]{0:T(1024)S(1)} %reshape.238, bf16[128,9,16,128]{3,2,1,0:T(8,128)(2,1)} %all-to-all-done.1), kind=kLoop, calls=%fused_computation.1 | loop fusion | flops 7077888 | bytes 9441792 | tf_op jit(solution)/shard_map/convert_element_type | solution.py:34
  232.7 7.1 %copy.139 = bf16[1152,16,128]{0,2,1:T(8,128)(2,1)} copy(bf16[1152,16,128]{2,1,0:T(8,128)(2,1)} %multiply_convert_fusion) | data formatting | bytes 9437184 | tf_op jit(solution)/shard_map/convert_element_type | solution.py:34
  239.8 9.6 %fusion.19 = f32[768,2048]{0,1:S(1)} fusion(bf16[1152,2048]{0,1:T(8,128)(2,1)} %bitcast.97, f32[1152,768]{0,1:T(8,128)} %convolution_bitcast_fusion.1, f32[1152,768]{0,1:T(8,128)} %convolution_bitcast_fusion), kind=kOutput, calls=%fused_computation.37 | convolution fusion | flops 3629187072 | bytes 18087936
  252.6 8.9 %convolution_convert_fusion.4 = bf16[16,128,768]{2,1,0:T(8,128)(2,1)} fusion(bf16[1152,16,128]{0,2,1:T(8,128)(2,1)} %copy.134, bf16[1152,768]{0,1:T(8,128)(2,1)} %get-tuple-element.41), kind=kOutput, calls=%fused_computation.29 | convolution fusion | flops 3625451520 | bytes 9633792 | tf_op jit(solution)/shard_map/dot_general | solution.py:13
  261.9 6.8 %gather_fusion = bf16[1024]{0:T(1024)(128)(2,1)S(1)} fusion(bf16[1152]{0:T(1024)(128)(2,1)S(1)} %reshape.234, s32[1024]{0:T(1024)S(1)} %broadcast_clamp_fusion), kind=kCustom, calls=%fused_computation | custom fusion | bytes 8192 | tf_op jit(solution)/shard_map/gather | solution.py:107
  269.8 12.9 %all-to-all-done.3 = bf16[128,9,16,128]{3,2,1,0:T(8,128)(2,1)} async-done(((bf16[128,9,16,128]{3,2,1,0:T(8,128)(2,1)}), bf16[128,9,16,128]{3,2,1,0:T(8,128)(2,1)}, u32[]{:S(2)}, u32[]{:S(2)}) %all-to-all-start.3) | async-done | bytes 4718624 | tf_op jit(solution)/shard_map/all_to_all | solution.py:99
  282.8 3.3 fusion
  288.7 5.4 %all-to-all-start.5 = ((bf16[128,17,128]{2,1,0:T(8,128)(2,1)}), bf16[128,17,128]{2,1,0:T(8,128)(2,1)S(1)}, u32[]{:S(2)}, u32[]{:S(2)}) async-start(bf16[128,17,128]{2,1,0:T(8,128)(2,1)} %fusion.32), calls=%async_computation.5 | async-start | bytes 1572864 | tf_op jit(solution)/shard_map/all_to_all | solution.py:119
  294.1 8.9 %convolution_convert_fusion.3 = bf16[16,128,768]{2,1,0:T(8,128)(2,1)} fusion(bf16[1152,16,128]{0,2,1:T(8,128)(2,1)} %copy.134, bf16[1152,768]{0,1:T(8,128)(2,1)} %get-tuple-element.42), kind=kOutput, calls=%fused_computation.28 | convolution fusion | flops 3625451520 | bytes 9633792 | tf_op jit(solution)/shard_map/dot_general | solution.py:13
  303.0 7.6 %all-to-all-done.5 = bf16[128,17,128]{2,1,0:T(8,128)(2,1)S(1)} async-done(((bf16[128,17,128]{2,1,0:T(8,128)(2,1)}), bf16[128,17,128]{2,1,0:T(8,128)(2,1)S(1)}, u32[]{:S(2)}, u32[]{:S(2)}) %all-to-all-start.5) | async-done | bytes 557088 | tf_op jit(solution)/shard_map/all_to_all | solution.py:119
  311.7 5.2 %all-to-all-start.6 = ((bf16[128,17,128]{2,1,0:T(8,128)(2,1)}), bf16[128,17,128]{2,1,0:T(8,128)(2,1)}, u32[]{:S(2)}, u32[]{:S(2)}) async-start(bf16[128,17,128]{2,1,0:T(8,128)(2,1)} %broadcast_in_dim.64), calls=%async_computation.6 | async-start | bytes 1572864 | tf_op jit(solution)/shard_map/all_to_all | solution.py:121
  317.0 2.9 fusion.28
  319.9 13.5 %all-to-all-done.6 = bf16[128,17,128]{2,1,0:T(8,128)(2,1)} async-done(((bf16[128,17,128]{2,1,0:T(8,128)(2,1)}), bf16[128,17,128]{2,1,0:T(8,128)(2,1)}, u32[]{:S(2)}, u32[]{:S(2)}) %all-to-all-start.6) | async-done | bytes 557088 | tf_op jit(solution)/shard_map/all_to_all | solution.py:121
  (75 shorter events, 27.3 us)
Async XLA Ops:
  0.6 135.3 %copy-start = (bf16[1,2048,768]{2,1,0:T(8,128)(2,1)S(1)}, bf16[1,2048,768]{2,1,0:T(8,128)(2,1)}, u32[]{:S(2)}) copy-start(bf16[1,2048,768]{2,1,0:T(8,128)(2,1)} %param.13) | copy-start | bytes 9437188
  0.6 7.4 %copy-start.7 = (s32[128,8]{0,1:T(8,128)S(1)}, s32[128,8]{0,1:T(8,128)}, u32[]{:S(2)}) copy-start(s32[128,8]{0,1:T(8,128)} %param.12) | copy-start | bytes 12292
  0.7 33.0 %copy-start.6 = (f32[2048]{0:T(1024)S(1)}, f32[2048]{0:T(1024)}, u32[]{:S(2)}) copy-start(f32[2048]{0:T(1024)} %param.9) | copy-start | bytes 24580
  5.5 0.8 copy-start.4
  17.6 32.7 %all-to-all-start = ((bf16[128,1,9]{2,1,0:T(2,128)(2,1)}), bf16[128,1,9]{2,1,0:T(2,128)(2,1)S(1)}, u32[]{:S(2)}, u32[]{:S(2)}) async-start(bf16[128,1,9]{2,1,0:T(2,128)(2,1)} %convert_element_type.154), calls=%async_computation | async-start | bytes 131072 | tf_op jit(solution)/shard_map/all_to_all | solution.py:89
  50.3 67.9 %all-to-all-start.2 = ((bf16[128,9,16,128]{3,2,1,0:T(8,128)(2,1)}), bf16[128,9,16,128]{3,2,1,0:T(8,128)(2,1)}, u32[]{:S(2)}, u32[]{:S(2)}) async-start(bf16[128,9,16,128]{3,2,1,0:T(8,128)(2,1)} %bitcast.94), calls=%async_computation.2 | async-start | bytes 9437184 | tf_op jit(solution)/shard_map/all_to_all | solution.py:87
  118.2 62.7 %all-to-all-start.1 = ((bf16[128,9,16,128]{3,2,1,0:T(8,128)(2,1)}), bf16[128,9,16,128]{3,2,1,0:T(8,128)(2,1)}, u32[]{:S(2)}, u32[]{:S(2)}) async-start(bf16[128,9,16,128]{3,2,1,0:T(8,128)(2,1)} %bitcast.93), calls=%async_computation.1 | async-start | bytes 9437184 | tf_op jit(solution)/shard_map/all_to_all | solution.py:88
  136.0 8.7 %copy-start.3 = (bf16[1152,16,128]{0,2,1:T(8,128)(2,1)S(1)}, bf16[1152,16,128]{0,2,1:T(8,128)(2,1)}, u32[]{:S(2)}) copy-start(bf16[1152,16,128]{0,2,1:T(8,128)(2,1)} %copy.134) | copy-start | bytes 14155780
  136.0 8.7 %copy-start.8 = (bf16[1,2048,768]{2,1,0:T(8,128)(2,1)S(1)}, bf16[1,2048,768]{2,1,0:T(8,128)(2,1)}, u32[]{:S(2)}) copy-start(bf16[1,2048,768]{2,1,0:T(8,128)(2,1)} %param.14) | copy-start | bytes 9437188
  194.8 20.2 %all-to-all-start.4 = ((bf16[128,1,9]{2,1,0:T(2,128)(2,1)}), bf16[128,1,9]{2,1,0:T(2,128)(2,1)S(1)}, u32[]{:S(2)}, u32[]{:S(2)}) async-start(bf16[128,1,9]{2,1,0:T(2,128)(2,1)} %convert_element_type.155), calls=%async_computation.4 | async-start | bytes 131072 | tf_op jit(solution)/shard_map/all_to_all | solution.py:102
  199.9 5.6 %copy-start.9 = (bf16[1,2048,768]{2,1,0:T(8,128)(2,1)S(1)}, bf16[1,2048,768]{2,1,0:T(8,128)(2,1)}, u32[]{:S(2)}) copy-start(bf16[1,2048,768]{2,1,0:T(8,128)(2,1)} %param.14) | copy-start | bytes 9437188
  215.0 67.7 %all-to-all-start.3 = ((bf16[128,9,16,128]{3,2,1,0:T(8,128)(2,1)}), bf16[128,9,16,128]{3,2,1,0:T(8,128)(2,1)}, u32[]{:S(2)}, u32[]{:S(2)}) async-start(bf16[128,9,16,128]{3,2,1,0:T(8,128)(2,1)} %bitcast.92), calls=%async_computation.3 | async-start | bytes 9437184 | tf_op jit(solution)/shard_map/all_to_all | solution.py:99
  261.9 7.5 %copy-start.2 = (bf16[128,2048]{1,0:T(8,128)(2,1)S(1)}, bf16[128,2048]{1,0:T(8,128)(2,1)}, u32[]{:S(2)}) copy-start(bf16[128,2048]{1,0:T(8,128)(2,1)} %param.8) | copy-start | bytes 1572868
  269.8 16.3 %copy-start.5 = (bf16[2048,128]{1,0:T(8,128)(2,1)S(1)}, bf16[2048,128]{1,0:T(8,128)(2,1)}, u32[]{:S(2)}) copy-start(bf16[2048,128]{1,0:T(8,128)(2,1)} %param.10) | copy-start | bytes 1572868
  288.7 21.8 %all-to-all-start.5 = ((bf16[128,17,128]{2,1,0:T(8,128)(2,1)}), bf16[128,17,128]{2,1,0:T(8,128)(2,1)S(1)}, u32[]{:S(2)}, u32[]{:S(2)}) async-start(bf16[128,17,128]{2,1,0:T(8,128)(2,1)} %fusion.32), calls=%async_computation.5 | async-start | bytes 1572864 | tf_op jit(solution)/shard_map/all_to_all | solution.py:119
  311.7 21.6 %all-to-all-start.6 = ((bf16[128,17,128]{2,1,0:T(8,128)(2,1)}), bf16[128,17,128]{2,1,0:T(8,128)(2,1)}, u32[]{:S(2)}, u32[]{:S(2)}) async-start(bf16[128,17,128]{2,1,0:T(8,128)(2,1)} %broadcast_in_dim.64), calls=%async_computation.6 | async-start | bytes 1572864 | tf_op jit(solution)/shard_map/all_to_all | solution.py:121
  317.0 20.6 %copy-start.1 = (bf16[1,2048,768]{2,1,0:T(8,128)(2,1)S(1)}, bf16[1,2048,768]{2,1,0:T(8,128)(2,1)}, u32[]{:S(2)}) copy-start(bf16[1,2048,768]{2,1,0:T(8,128)(2,1)} %param.13) | copy-start | bytes 9437188
